TPU v7x, 128 devices: a whole 4x4x4 slice. The times are simulated.
128 devices in a mesh: rows: 8 (over y, z_lo), pairs: 16 (over z_hi, x, core).
Axes of the slice: x: 4, y: 4, z: 4 (z_hi: 2, z_lo: 2; z = z_hi * 2 + z_lo), core: 2. Of those that a mesh axis runs over, the one named last changes fastest.
Arguments:
- unit_rows: float32 [8, 16, 192, 8192], P('rows', 'pairs'), may hold values from -6 to 6
- unit_counts: int32 [8, 16], P('rows'), may hold values from 1 to 192, 1024 in all within a row
- seating: int32 [32], replicated, may hold values from 0 to 31, each once
- channel_scale: float32 [8192], replicated, may hold values from 0.25 to 4
Outputs:
- rotated: float32 [8192, 8192], P('rows', 'pairs')
Inputs may be any that keep to these rules, and one draw needn't show every extreme that they name: `unit_counts`: each row of 16 counts sums to 1024, and in each row the largest is exactly 192. `seating`: each block once.
All inputs are finite; a program needn't handle non-finite values.
Results may differ from a plain program's by a relative error of at most 0.0001.
Values sent between devices are 32-bit elements; how exact they have to be, the bound alone decides.
No kernel may reach another device: no remote copies, remote signals or barrier semaphores. Data moves between devices by JAX's collectives and lax.ppermute only.
A program may use at most 128 MiB of HBM per device.

v0:
```python
import jax
import jax.numpy as jnp
from jax import lax
from jax.experimental import pallas as pl
from jax.experimental.pallas import tpu as pltpu
from jax.sharding import PartitionSpec as P

ROWS_DEV = 1024
BLOCK = 256


epsilon = 1e-06
HI = lax.Precision.HIGHEST
BIG = lax.Precision.HIGH
NEWTON_TOL_SQ = 1e-6
NEWTON_MAX = 60


def passed_along(array, axis, by):
    length = lax.axis_size(axis)
    pairs = [(i, i + by) for i in range(length) if 0 <= i + by < length]
    return lax.ppermute(array, axis, pairs)


def spd_inverse(sym_part):
    n = sym_part.shape[0]
    identity = jnp.eye(n, dtype=jnp.float32)
    spread = jnp.sqrt(jnp.sum((sym_part - identity) ** 2))
    scale = jnp.where(spread < 1.0, 1.0, 2.0 / (2.0 + spread))
    start = identity - scale * sym_part
    inverse = scale * (identity + start)
    residual = lax.optimization_barrier(jnp.dot(start, start, precision=BIG))
    err = jnp.sum(residual * residual)

    def cond(state):
        step, _, _, err = state
        return jnp.logical_and(err > NEWTON_TOL_SQ, step < NEWTON_MAX)

    def body(state):
        step, inverse, residual, _ = state
        inverse = inverse + jnp.dot(inverse, residual, precision=HI)
        residual = identity - jnp.dot(sym_part, inverse, precision=HI)
        return step + 1, inverse, residual, jnp.sum(residual * residual)

    state = (jnp.int32(1), inverse, residual, err)
    _, inverse, residual, _ = lax.while_loop(cond, body, state)
    return inverse + jnp.dot(inverse, residual, precision=BIG)


def row_sum(partial, axis):
    count = lax.axis_size(axis)
    rows, cols = partial.shape
    pieces = lax.all_to_all(partial.reshape(count, rows // count, cols), axis, 0, 0, tiled=False)
    block = jnp.sum(pieces, axis=0)
    spread = jnp.broadcast_to(block[None], (count, rows // count, cols))
    return lax.all_to_all(spread, axis, 0, 0, tiled=False).reshape(rows, cols)


def seat_kernel(seat_ref, *refs):
    count = (len(refs) - 1) // 2
    blocks, scales, out_ref = refs[:count], refs[count:2 * count], refs[-1]
    for k in range(count):
        out_ref[k // 2, :, (k % 2) * BLOCK:(k % 2 + 1) * BLOCK] = blocks[k][...] * scales[k][...]


def seat_and_scale(rows, scale, seating):
    capacity, columns = rows.shape
    pairs = columns // (2 * BLOCK)
    step_pairs = 8
    seats = 2 * step_pairs
    block_of = lambda k: (lambda q, seat: (0, seat[seats * q + k]))
    return pl.pallas_call(
        seat_kernel,
        out_shape=jax.ShapeDtypeStruct((pairs, capacity, 2 * BLOCK), jnp.float32),
        grid_spec=pltpu.PrefetchScalarGridSpec(
            num_scalar_prefetch=1,
            grid=(pairs // step_pairs,),
            in_specs=[pl.BlockSpec((capacity, BLOCK), block_of(k)) for k in range(seats)]
            + [pl.BlockSpec((1, BLOCK), block_of(k)) for k in range(seats)],
            out_specs=pl.BlockSpec((step_pairs, capacity, 2 * BLOCK), lambda q, seat: (q, 0, 0)),
        ),
    )(seating, *([rows] * seats), *([scale.reshape(1, columns)] * seats))


def row_gather_sum(partial, axis):
    count = lax.axis_size(axis)
    spread = jnp.broadcast_to(partial[None], (count,) + partial.shape)
    return jnp.sum(lax.all_to_all(spread, axis, 0, 0, tiled=False), axis=0)


def cayley(gram_full):
    identity = jnp.eye(gram_full.shape[0], dtype=jnp.float32)
    diag_terms = jnp.sum(gram_full * identity, axis=0)
    skew_part = (
        gram_full
        * (diag_terms[None, :] - diag_terms[:, None])
        / (2.0 * (diag_terms[:, None] ** 2 + diag_terms[None, :] ** 2) + epsilon)
    )
    skew_square = jnp.dot(skew_part, skew_part, precision=BIG)
    numerator = identity + skew_part + 0.25 * skew_square
    sym_part = identity - 0.25 * skew_square
    return jnp.dot(numerator, spd_inverse(sym_part), precision=BIG)


def first_round(panels):
    partial_gram = lax.dot_general(
        panels,
        panels,
        (((0,), (0,)), ((), ())),
        precision=BIG,
        preferred_element_type=jnp.float32,
    )
    gram_full = row_sum(partial_gram, "rows")
    rotation = cayley(gram_full)
    turned = jnp.dot(panels, rotation, precision=BIG)
    gram_turned = jnp.dot(gram_full, rotation, precision=BIG)
    half_width = panels.shape[1] // 2
    block_gram = lambda cut: lax.dot_general(
        rotation[:, cut], gram_turned[:, cut], (((0,), (0,)), ((), ())), precision=BIG
    )
    return turned, block_gram(slice(0, half_width)), block_gram(slice(half_width, None))


def advance(panels, upper_gram, lower_gram):
    half_width = panels.shape[1] // 2
    upper = panels[:, :half_width]
    lower = panels[:, half_width:]
    pair_index = lax.axis_index("pairs")
    last_pair = lax.axis_size("pairs") - 1
    first = pair_index == 0
    last = pair_index == last_pair
    came_up = passed_along(jnp.where(first, lower, upper), "pairs", 1)
    came_down = passed_along(lower, "pairs", -1)
    gram_up = passed_along(jnp.where(first, lower_gram, upper_gram), "pairs", 1)
    gram_down = passed_along(lower_gram, "pairs", -1)
    new_upper = jnp.where(first, upper, came_up)
    new_upper_gram = jnp.where(first, upper_gram, gram_up)
    new_lower = jnp.where(last, upper, came_down)
    new_lower_gram = jnp.where(last, upper_gram, gram_down)
    return new_upper, new_lower, new_upper_gram, new_lower_gram


def second_round(upper, lower, upper_gram, lower_gram):
    partial_cross = lax.dot_general(
        upper,
        lower,
        (((0,), (0,)), ((), ())),
        precision=BIG,
        preferred_element_type=jnp.float32,
    )
    cross = row_gather_sum(partial_cross, "rows")
    gram_full = jnp.concatenate(
        [
            jnp.concatenate([upper_gram, cross], axis=1),
            jnp.concatenate([cross.T, lower_gram], axis=1),
        ],
        axis=0,
    )
    rotation = cayley(gram_full)
    half_width = upper.shape[1]
    return jnp.dot(upper, rotation[:half_width], precision=BIG) + jnp.dot(
        lower, rotation[half_width:], precision=BIG
    )


def compact(panels, group_counts, capacity):
    unit_ends = jnp.cumsum(group_counts)
    target = lax.iota(jnp.int32, ROWS_DEV)
    passed = (target[:, None] >= unit_ends[None, :]).astype(jnp.int32)
    owner_unit = jnp.sum(passed, axis=1)
    owner_start = jnp.sum(passed * group_counts[None, :], axis=1)
    source = owner_unit * capacity + target - owner_start
    return jnp.take(panels, source, axis=0, mode="clip")


def local(unit_rows, unit_counts, seating, channel_scale):
    capacity = unit_rows.shape[2]
    group_counts = unit_counts[0]
    seated = seat_and_scale(unit_rows[0, 0], channel_scale, seating)
    panels = lax.all_to_all(seated, "pairs", 0, 0, tiled=True)
    current = compact(panels.reshape(-1, 2 * BLOCK), group_counts, capacity)
    return second_round(*advance(*first_round(current)))


def solution(mesh):
    return jax.shard_map(
        local,
        mesh=mesh,
        in_specs=(P("rows", "pairs", None, None), P("rows", None), P(), P()),
        out_specs=P("rows", "pairs"),
        check_vma=False,
    )
```

profile of v0, /device:TPU:3, one launch (start us, length us, event | category | flops | bytes accessed | tf_op | source)
XLA Modules:
  0.0 295.9 jit_solution(17391406041595330233)
XLA Ops:
  0.0 6.0 %shard_map.46 = f32[16,192,512]{2,1,0:T(8,128)} custom-call(s32[32]{0:T(128)} %seat_ref.1, f32[192,8192]{1,0:T(8,128)} %bitcast.58, f32[192,8192]{1,0:T(8,128)} %bitcast.59, f32[192,8192]{1,0:T(8,128)} %bitcast.60, f32[192,8192]{1,0:T(8,128)} %bitcast.61, f32[192,8192]{1,0:T(8,128)} %bitcast.62, f32[192,8192]{1,0:T(8,128)} %bitcast.63, ...), custom_call_target="tpu_custom_call" | custom-call | tf_op jit(solution)/shard_map/pallas_call | solution.py:72
  6.0 8.5 %all-to-all-start = ((f32[16,192,512]{2,1,0:T(8,128)}), f32[16,192,512]{2,1,0:T(8,128)}, u32[]{:S(2)}, u32[]{:S(2)}) async-start(f32[16,192,512]{2,1,0:T(8,128)} %shard_map.46), calls=%async_computation | async-start | bytes 12582912 | tf_op jit(solution)/shard_map/all_to_all | solution.py:180
  14.9 84.8 %all-to-all-done = f32[16,192,512]{2,1,0:T(8,128)} async-done(((f32[16,192,512]{2,1,0:T(8,128)}), f32[16,192,512]{2,1,0:T(8,128)}, u32[]{:S(2)}, u32[]{:S(2)}) %all-to-all-start) | async-done | bytes 6291488 | tf_op jit(solution)/shard_map/all_to_all | solution.py:180
  99.7 6.8 %gather_fusion = f32[1024,512]{1,0:T(8,128)S(1)} fusion(f32[3072,512]{1,0:T(8,128)} %bitcast.2, s32[1024]{0:T(1024)S(1)} %broadcast_clamp_fusion), kind=kCustom, calls=%fused_computation | custom fusion | bytes 4198400 | tf_op jit(solution)/shard_map/jit(_take)/gather | solution.py:173
  106.5 1.8 fusion.47
  108.4 18.8 %all_to_all.20 = f32[8,64,512]{2,1,0:T(8,128)S(1)} all-to-all(f32[8,64,512]{2,1,0:T(8,128)S(1)} %bitcast.93), channel_id=1, replica_groups=mesh['rows'=8,'pairs'=16] {'rows'}, dimensions={0} | all-to-all | bytes 2097152 | tf_op jit(solution)/shard_map/all_to_all | solution.py:53
  127.3 1.1 broadcast_in_dim.6
  128.4 3.6 %all-to-all-start.2 = ((f32[8,64,512]{2,1,0:T(8,128)}), f32[8,64,512]{2,1,0:T(8,128)S(1)}, u32[]{:S(2)}, u32[]{:S(2)}) async-start(f32[8,64,512]{2,1,0:T(8,128)} %broadcast_in_dim.6), calls=%async_computation.2 | async-start | bytes 2097152 | tf_op jit(solution)/shard_map/all_to_all | solution.py:56
  132.0 14.1 %all-to-all-done.2 = f32[8,64,512]{2,1,0:T(8,128)S(1)} async-done(((f32[8,64,512]{2,1,0:T(8,128)}), f32[8,64,512]{2,1,0:T(8,128)S(1)}, u32[]{:S(2)}, u32[]{:S(2)}) %all-to-all-start.2) | async-done | bytes 1048608 | tf_op jit(solution)/shard_map/all_to_all | solution.py:56
  146.3 0.3 add_divide_fusion.1
  146.6 0.4 copy-done.4
  147.0 1.9 convert_subtract_fusion.5
  149.7 1.1 fusion.24
  150.8 1.0 copy-done.9
  151.8 0.9 fusion.11
  152.7 1.6 copy.18
  154.3 27.6 %while.30 = (s32[]{:T(128)}, f32[512,512]{1,0:T(8,128)S(1)}, f32[512,512]{0,1:T(8,128)S(1)}, f32[]{:T(128)}, f32[512,512]{1,0:T(8,128)S(1)}, /*index=5*/s32[]{:T(128)}) while((s32[]{:T(128)}, f32[512,512]{1,0:T(8,128)S(1)}, f32[512,512]{0,1:T(8,128)S(1)}, f32[]{:T(128)}, f32[512,512]{1,0:T(8,128)S(1)}, /*index=5*/s32[]{:T(128)}) %tuple.58), condition=%wide.region_9.10_spmd.clone, body=%wide.region_7.9_spmd.clone.sunk | while | flops 3222798336 | bytes 8388693 | solution.py:46
  155.2 1.9 convolution_add_fusion.7
  157.0 4.1 %multiply_reduce_fusion.6 = (f32[]{:T(128)}, f32[512,512]{0,1:T(8,128)S(1)}) fusion(f32[512,512]{1,0:T(8,128)S(1)} %convolution_add_fusion.7, f32[512,512]{1,0:T(8,128)S(1)} %get-tuple-element.253), kind=kOutput, calls=%fused_computation.7.clone.1 | convolution fusion | flops 1611923456 | bytes 3145732 | tf_op jit(solution)/shard_map/while/body/dot_general | solution.py:42
  161.9 1.9 convolution_add_fusion.7
  163.7 4.1 %multiply_reduce_fusion.6 = (f32[]{:T(128)}, f32[512,512]{0,1:T(8,128)S(1)}) fusion(f32[512,512]{1,0:T(8,128)S(1)} %convolution_add_fusion.7, f32[512,512]{1,0:T(8,128)S(1)} %get-tuple-element.253), kind=kOutput, calls=%fused_computation.7.clone.1 | convolution fusion | flops 1611923456 | bytes 3145732 | tf_op jit(solution)/shard_map/while/body/dot_general | solution.py:42
  168.6 1.9 convolution_add_fusion.7
  170.5 4.1 %multiply_reduce_fusion.6 = (f32[]{:T(128)}, f32[512,512]{0,1:T(8,128)S(1)}) fusion(f32[512,512]{1,0:T(8,128)S(1)} %convolution_add_fusion.7, f32[512,512]{1,0:T(8,128)S(1)} %get-tuple-element.253), kind=kOutput, calls=%fused_computation.7.clone.1 | convolution fusion | flops 1611923456 | bytes 3145732 | tf_op jit(solution)/shard_map/while/body/dot_general | solution.py:42
  175.3 1.9 convolution_add_fusion.7
  177.2 4.1 %multiply_reduce_fusion.6 = (f32[]{:T(128)}, f32[512,512]{0,1:T(8,128)S(1)}) fusion(f32[512,512]{1,0:T(8,128)S(1)} %convolution_add_fusion.7, f32[512,512]{1,0:T(8,128)S(1)} %get-tuple-element.253), kind=kOutput, calls=%fused_computation.7.clone.1 | convolution fusion | flops 1611923456 | bytes 3145732 | tf_op jit(solution)/shard_map/while/body/dot_general | solution.py:42
  181.9 1.1 convolution_add_fusion.4
  183.1 0.3 copy-done.8
  183.5 1.3 fusion.7
  185.1 1.8 fusion.48
  186.9 1.7 fusion.46
  188.5 3.8 %collective-permute-start = (f32[1024,256]{1,0:T(8,128)}, f32[1024,256]{1,0:T(8,128)}, u32[]{:S(2)}, u32[]{:S(2)}) collective-permute-start(f32[1024,256]{1,0:T(8,128)} %get-tuple-element.156), channel_id=1, source_target_pairs={{0,1},{1,2},{2,3},{3,4},{4,5},{5,6},{6,7},{7,8},{8,9},{9,10},{10,1... | collective-permute-start | bytes 3145736 | tf_op jit(solution)/shard_map/ppermute | solution.py:22
  192.3 2.4 collective-permute-start.2
  194.8 9.6 %collective-permute-done = f32[1024,256]{1,0:T(8,128)} collective-permute-done((f32[1024,256]{1,0:T(8,128)}, f32[1024,256]{1,0:T(8,128)}, u32[]{:S(2)}, u32[]{:S(2)}) %collective-permute-start) | collective-permute-done | bytes 1048608 | tf_op jit(solution)/shard_map/ppermute | solution.py:22
  204.4 4.4 %collective-permute-done.2 = f32[1024,256]{1,0:T(8,128)} collective-permute-done((f32[1024,256]{1,0:T(8,128)}, f32[1024,256]{1,0:T(8,128)}, u32[]{:S(2)}, u32[]{:S(2)}) %collective-permute-start.2) | collective-permute-done | bytes 1048608 | tf_op jit(solution)/shard_map/ppermute | solution.py:22
  208.8 2.5 fusion.43
  211.3 1.5 broadcast_in_dim.7
  212.8 4.7 %all-to-all-start.3 = ((f32[8,256,256]{2,1,0:T(8,128)}), f32[8,256,256]{2,1,0:T(8,128)}, u32[]{:S(2)}, u32[]{:S(2)}) async-start(f32[8,256,256]{2,1,0:T(8,128)} %broadcast_in_dim.7), calls=%async_computation.3 | async-start | bytes 4194304 | tf_op jit(solution)/shard_map/all_to_all | solution.py:88
  217.6 1.0 fusion.49
  218.6 0.6 fusion.32
  219.2 0.6 broadcast_select_fusion.2
  219.8 1.9 collective-permute-start.1
  221.7 2.4 collective-permute-start.3
  224.1 0.9 collective-permute-done.1
  225.0 4.8 %collective-permute-done.3 = f32[256,256]{1,0:T(8,128)S(1)} collective-permute-done((f32[256,256]{1,0:T(8,128)S(1)}, f32[256,256]{1,0:T(8,128)S(1)}, u32[]{:S(2)}, u32[]{:S(2)}) %collective-permute-start.3) | collective-permute-done | bytes 262176 | tf_op jit(solution)/shard_map/ppermute | solution.py:22
  229.9 18.9 %all-to-all-done.3 = f32[8,256,256]{2,1,0:T(8,128)} async-done(((f32[8,256,256]{2,1,0:T(8,128)}), f32[8,256,256]{2,1,0:T(8,128)}, u32[]{:S(2)}, u32[]{:S(2)}) %all-to-all-start.3) | async-done | bytes 2097184 | tf_op jit(solution)/shard_map/all_to_all | solution.py:88
  248.8 1.8 reduce_sum.117
  250.8 2.2 convert_subtract_fusion.2
  254.0 2.1 fusion.25
  256.0 1.6 copy.23
  257.6 2.1 multiply_reduce_fusion.2
  259.7 27.3 %while.31 = (s32[]{:T(128)}, f32[512,512]{1,0:T(8,128)S(1)}, f32[512,512]{0,1:T(8,128)S(1)}, f32[]{:T(128)}, f32[512,512]{1,0:T(8,128)S(1)}, /*index=5*/s32[]{:T(128)}) while((s32[]{:T(128)}, f32[512,512]{1,0:T(8,128)S(1)}, f32[512,512]{0,1:T(8,128)S(1)}, f32[]{:T(128)}, f32[512,512]{1,0:T(8,128)S(1)}, ...), condition=%wide.region_16.17_spmd.clone, body=%wide.region_14.16_spmd.clone.sunk | while | flops 3222798336 | bytes 8388693 | solution.py:46
  260.3 1.9 convolution_add_fusion.8
  262.2 4.1 %multiply_reduce_fusion.7 = (f32[]{:T(128)}, f32[512,512]{0,1:T(8,128)S(1)}) fusion(f32[512,512]{1,0:T(8,128)S(1)} %convolution_add_fusion.8, f32[512,512]{1,0:T(8,128)S(1)} %get-tuple-element.271), kind=kOutput, calls=%fused_computation.12.clone.1 | convolution fusion | flops 1611923456 | bytes 3145732 | tf_op jit(solution)/shard_map/while/body/dot_general | solution.py:42
  267.0 1.9 convolution_add_fusion.8
  268.8 4.1 %multiply_reduce_fusion.7 = (f32[]{:T(128)}, f32[512,512]{0,1:T(8,128)S(1)}) fusion(f32[512,512]{1,0:T(8,128)S(1)} %convolution_add_fusion.8, f32[512,512]{1,0:T(8,128)S(1)} %get-tuple-element.271), kind=kOutput, calls=%fused_computation.12.clone.1 | convolution fusion | flops 1611923456 | bytes 3145732 | tf_op jit(solution)/shard_map/while/body/dot_general | solution.py:42
  273.6 1.9 convolution_add_fusion.8
  275.5 4.1 %multiply_reduce_fusion.7 = (f32[]{:T(128)}, f32[512,512]{0,1:T(8,128)S(1)}) fusion(f32[512,512]{1,0:T(8,128)S(1)} %convolution_add_fusion.8, f32[512,512]{1,0:T(8,128)S(1)} %get-tuple-element.271), kind=kOutput, calls=%fused_computation.12.clone.1 | convolution fusion | flops 1611923456 | bytes 3145732 | tf_op jit(solution)/shard_map/while/body/dot_general | solution.py:42
  280.2 1.9 convolution_add_fusion.8
  282.1 4.1 %multiply_reduce_fusion.7 = (f32[]{:T(128)}, f32[512,512]{0,1:T(8,128)S(1)}) fusion(f32[512,512]{1,0:T(8,128)S(1)} %convolution_add_fusion.8, f32[512,512]{1,0:T(8,128)S(1)} %get-tuple-element.271), kind=kOutput, calls=%fused_computation.12.clone.1 | convolution fusion | flops 1611923456 | bytes 3145732 | tf_op jit(solution)/shard_map/while/body/dot_general | solution.py:42
  287.1 1.1 convolution_add_fusion.3
  288.4 1.3 fusion.14
  289.7 0.3 copy-done.3
  290.0 2.2 fusion.26
  292.3 3.6 %convolution_add_fusion.2 = f32[1024,512]{1,0:T(8,128)} fusion(f32[1024,512]{1,0:T(8,128)S(1)} %fusion.26, f32[512,512]{1,0:T(8,128)S(1)} %fusion.14, f32[1024,256]{1,0:T(8,128)} %collective-permute-done, f32[1024,512]{1,0:T(8,128)S(1)} %copy-done.3, pred[]{:T(512)S(6)} %eq.39), kind=kOutput, calls=%fused_computation.23 | convolution fusion | flops 806092800 | bytes 6815745 | tf_op jit(solution)/shard_map/dot_general | solution.py:161
  (60 shorter events, 2.5 us)
Async XLA Ops:
  6.0 8.5 %copy-start.18 = (s32[1,16]{1,0:T(1,128)S(1)}, s32[1,16]{1,0:T(1,128)}, u32[]{:S(2)}) copy-start(s32[1,16]{1,0:T(1,128)} %param.9) | copy-start | bytes 196
  6.0 93.7 %all-to-all-start = ((f32[16,192,512]{2,1,0:T(8,128)}), f32[16,192,512]{2,1,0:T(8,128)}, u32[]{:S(2)}, u32[]{:S(2)}) async-start(f32[16,192,512]{2,1,0:T(8,128)} %shard_map.46), calls=%async_computation | async-start | bytes 12582912 | tf_op jit(solution)/shard_map/all_to_all | solution.py:180
  106.5 1.9 copy-start
  128.4 17.6 %all-to-all-start.2 = ((f32[8,64,512]{2,1,0:T(8,128)}), f32[8,64,512]{2,1,0:T(8,128)S(1)}, u32[]{:S(2)}, u32[]{:S(2)}) async-start(f32[8,64,512]{2,1,0:T(8,128)} %broadcast_in_dim.6), calls=%async_computation.2 | async-start | bytes 2097152 | tf_op jit(solution)/shard_map/all_to_all | solution.py:56
  146.0 1.0 copy-start.4
  148.9 1.9 copy-start.7
  150.8 1.0 copy-start.9
  181.9 1.2 copy-start.5
  181.9 1.5 copy-start.8
  183.5 1.6 copy-start.1
  186.9 21.9 %copy-start.2 = (f32[1024,512]{1,0:T(8,128)}, f32[1024,512]{1,0:T(8,128)S(1)}, u32[]{:S(2)}) copy-start(f32[1024,512]{1,0:T(8,128)S(1)} %fusion.48) | copy-start | bytes 6291460
  188.5 15.8 %collective-permute-start = (f32[1024,256]{1,0:T(8,128)}, f32[1024,256]{1,0:T(8,128)}, u32[]{:S(2)}, u32[]{:S(2)}) collective-permute-start(f32[1024,256]{1,0:T(8,128)} %get-tuple-element.156), channel_id=1, source_target_pairs={{0,1},{1,2},{2,3},{3,4},{4,5},{5,6},{6,7},{7,8},{8,9},{9,10},{10,1... | collective-permute-start | bytes 3145736 | tf_op jit(solution)/shard_map/ppermute | solution.py:22
  192.3 16.4 %collective-permute-start.2 = (f32[1024,256]{1,0:T(8,128)}, f32[1024,256]{1,0:T(8,128)}, u32[]{:S(2)}, u32[]{:S(2)}) collective-permute-start(f32[1024,256]{1,0:T(8,128)} %get-tuple-element.155), channel_id=1, source_target_pairs={{1,0},{2,1},{3,2},{4,3},{5,4},{6,5},{7,6},{8,7},{9,8},{10,9},{11,1... | collective-permute-start | bytes 3145736 | tf_op jit(solution)/shard_map/ppermute | solution.py:22
  212.8 4.7 %copy-start.6 = (f32[8,64,512]{2,1,0:T(8,128)S(1)}, f32[8,64,512]{2,1,0:T(8,128)}, u32[]{:S(2)}) copy-start(f32[8,64,512]{2,1,0:T(8,128)} %copy-done.4) | copy-start | bytes 3145732
  212.8 36.0 %all-to-all-start.3 = ((f32[8,256,256]{2,1,0:T(8,128)}), f32[8,256,256]{2,1,0:T(8,128)}, u32[]{:S(2)}, u32[]{:S(2)}) async-start(f32[8,256,256]{2,1,0:T(8,128)} %broadcast_in_dim.7), calls=%async_computation.3 | async-start | bytes 4194304 | tf_op jit(solution)/shard_map/all_to_all | solution.py:88
  219.8 5.2 %collective-permute-start.1 = (f32[256,256]{1,0:T(8,128)S(1)}, f32[256,256]{1,0:T(8,128)S(1)}, u32[]{:S(2)}, u32[]{:S(2)}) collective-permute-start(f32[256,256]{1,0:T(8,128)S(1)} %get-tuple-element.164), channel_id=1, source_target_pairs={{0,1},{1,2},{2,3},{3,4},{4,5},{5,6},{6,7},{7,8},{8,9},{9,10},{10,1... | collective-permute-start | bytes 786440 | tf_op jit(solution)/shard_map/ppermute | solution.py:22
  221.7 8.1 %collective-permute-start.3 = (f32[256,256]{1,0:T(8,128)S(1)}, f32[256,256]{1,0:T(8,128)S(1)}, u32[]{:S(2)}, u32[]{:S(2)}) collective-permute-start(f32[256,256]{1,0:T(8,128)S(1)} %get-tuple-element.165), channel_id=1, source_target_pairs={{1,0},{2,1},{3,2},{4,3},{5,4},{6,5},{7,6},{8,7},{9,8},{10,9},{11,1... | collective-permute-start | bytes 786440 | tf_op jit(solution)/shard_map/ppermute | solution.py:22
  229.9 23.1 %copy-start.14 = (f32[256,256]{1,0:T(8,128)}, f32[256,256]{1,0:T(8,128)S(1)}, u32[]{:S(2)}) copy-start(f32[256,256]{1,0:T(8,128)S(1)} %get-tuple-element.161) | copy-start | bytes 786436
  229.9 23.1 %copy-start.16 = (f32[256,256]{1,0:T(8,128)}, f32[256,256]{1,0:T(8,128)S(1)}, u32[]{:S(2)}) copy-start(f32[256,256]{1,0:T(8,128)S(1)} %get-tuple-element.162) | copy-start | bytes 786436
  250.7 2.3 copy-start.12
  253.0 1.0 copy-start.10
  287.0 1.2 copy-start.11
  287.0 1.3 copy-start.13
  287.0 1.3 copy-start.15
  287.0 1.4 copy-start.17
  288.4 1.6 copy-start.3
where the time goes:
time: 301 us; the launch traced here: 296 us
  waiting for transfers between devices  137 us (46%)
  matrix products  74 us (25%)
  starting transfers between devices  27.3 us (9%)
  blocking collectives  18.8 us (6%)
  local copies, waits for them, and re-layouts  16.3 us (5%)
  other arithmetic  7.58 us (3%)
  loops' own time  6.58 us (2%)
  Pallas kernels  6.03 us (2%)
    all_to_all x1, waiting for transfers between devices, local(): panels = lax.all_to_all(seated, 'pairs', 0, 0, tiled=True)  84.8 us
    dot_general x8, matrix products, body(): residual = identity - jnp.dot(sym_part, inverse, precision=HI)  32.9 us
    ppermute x4, waiting for transfers between devices, passed_along(): return lax.ppermute(array, axis, pairs)  19.7 us
    all_to_all x1, waiting for transfers between devices, row_gather_sum(): return jnp.sum(lax.all_to_all(spread, axis, 0, 0, tiled=False), axis=0)  18.9 us
    all_to_all x1, blocking collectives, row_sum(): lax.all_to_all(partial.reshape(count, rows // count, cols), axis, 0, 0, t...  18.8 us
    dot_general x8, matrix products, body(): inverse = inverse + jnp.dot(inverse, residual, precision=HI)  14.9 us
    all_to_all x1, waiting for transfers between devices, row_sum(): return lax.all_to_all(spread, axis, 0, 0, tiled=False).reshape(rows, cols)  14.1 us
    ppermute x4, starting transfers between devices, passed_along(): return lax.ppermute(array, axis, pairs)  10.5 us
  transfers between devices with their start and end apart: 7, of which 7 were waited for; matrix products, arithmetic and copies ran while one was open for 1% of the time, Pallas kernels for 0%

commit v1 on v0

--- a/solution.py
+++ b/solution.py
@@ -38,7 +38,7 @@
 
     def body(state):
         step, inverse, residual, _ = state
-        inverse = inverse + jnp.dot(inverse, residual, precision=HI)
+        inverse = inverse + jnp.dot(inverse, residual, precision=BIG)
         residual = identity - jnp.dot(sym_part, inverse, precision=HI)
         return step + 1, inverse, residual, jnp.sum(residual * residual)
 
@@ -99,7 +99,7 @@
     skew_square = jnp.dot(skew_part, skew_part, precision=BIG)
     numerator = identity + skew_part + 0.25 * skew_square
     sym_part = identity - 0.25 * skew_square
-    return jnp.dot(numerator, spd_inverse(sym_part), precision=BIG)
+    return jnp.dot(numerator, spd_inverse(sym_part), precision=HI)
 
 
 def first_round(panels):

time: 301 us -> 297 us (0.987); the launches traced: 296 us -> 296 us
    dot_general x8 -> x9, matrix products: 32.9 us -> 37 us  [body(): residual = identity - jnp.dot(sym_part, inverse, precision=HI)]
    dot_general x10 -> x11, matrix products: 17.4 us -> 13.6 us  [the longest x9 9.29 us: body(): inverse = inverse + jnp.dot(inverse, residual, precision=BIG)]
where the time goes in v1:
time: 297 us; the launch traced here: 296 us
  waiting for transfers between devices  137 us (46%)
  matrix products  74.3 us (25%)
  starting transfers between devices  27.3 us (9%)
  blocking collectives  18.8 us (6%)
  local copies, waits for them, and re-layouts  15.7 us (5%)
  other arithmetic  7.58 us (3%)
  loops' own time  7.18 us (2%)
  Pallas kernels  6.03 us (2%)
    all_to_all x1, waiting for transfers between devices, local(): panels = lax.all_to_all(seated, 'pairs', 0, 0, tiled=True)  84.8 us
    dot_general x9, matrix products, body(): residual = identity - jnp.dot(sym_part, inverse, precision=HI)  37 us
    ppermute x4, waiting for transfers between devices, passed_along(): return lax.ppermute(array, axis, pairs)  19.7 us
    all_to_all x1, waiting for transfers between devices, row_gather_sum(): return jnp.sum(lax.all_to_all(spread, axis, 0, 0, tiled=False), axis=0)  18.9 us
    all_to_all x1, blocking collectives, row_sum(): lax.all_to_all(partial.reshape(count, rows // count, cols), axis, 0, 0, t...  18.8 us
    all_to_all x1, waiting for transfers between devices, row_sum(): return lax.all_to_all(spread, axis, 0, 0, tiled=False).reshape(rows, cols)  14.1 us
    ppermute x4, starting transfers between devices, passed_along(): return lax.ppermute(array, axis, pairs)  10.5 us
    dot_general x9, matrix products, body(): inverse = inverse + jnp.dot(inverse, residual, precision=BIG)  9.29 us
  transfers between devices with their start and end apart: 7, of which 7 were waited for; matrix products, arithmetic and copies ran while one was open for 1% of the time, Pallas kernels for 0%

profile of v1, /device:TPU:3, one launch (start us, length us, event | category | flops | bytes accessed | tf_op | source)
XLA Modules:
  0.0 296.3 jit_solution(8898935488330647909)
XLA Ops:
  0.0 6.0 %shard_map.46 = f32[16,192,512]{2,1,0:T(8,128)} custom-call(s32[32]{0:T(128)} %seat_ref.1, f32[192,8192]{1,0:T(8,128)} %bitcast.58, f32[192,8192]{1,0:T(8,128)} %bitcast.59, f32[192,8192]{1,0:T(8,128)} %bitcast.60, f32[192,8192]{1,0:T(8,128)} %bitcast.61, f32[192,8192]{1,0:T(8,128)} %bitcast.62, f32[192,8192]{1,0:T(8,128)} %bitcast.63, ...), custom_call_target="tpu_custom_call" | custom-call | tf_op jit(solution)/shard_map/pallas_call | solution.py:72
  6.0 8.5 %all-to-all-start = ((f32[16,192,512]{2,1,0:T(8,128)}), f32[16,192,512]{2,1,0:T(8,128)}, u32[]{:S(2)}, u32[]{:S(2)}) async-start(f32[16,192,512]{2,1,0:T(8,128)} %shard_map.46), calls=%async_computation | async-start | bytes 12582912 | tf_op jit(solution)/shard_map/all_to_all | solution.py:180
  14.9 84.8 %all-to-all-done = f32[16,192,512]{2,1,0:T(8,128)} async-done(((f32[16,192,512]{2,1,0:T(8,128)}), f32[16,192,512]{2,1,0:T(8,128)}, u32[]{:S(2)}, u32[]{:S(2)}) %all-to-all-start) | async-done | bytes 6291488 | tf_op jit(solution)/shard_map/all_to_all | solution.py:180
  99.7 6.8 %gather_fusion = f32[1024,512]{1,0:T(8,128)S(1)} fusion(f32[3072,512]{1,0:T(8,128)} %bitcast.2, s32[1024]{0:T(1024)S(1)} %broadcast_clamp_fusion), kind=kCustom, calls=%fused_computation | custom fusion | bytes 4198400 | tf_op jit(solution)/shard_map/jit(_take)/gather | solution.py:173
  106.5 1.8 fusion.47
  108.4 18.8 %all_to_all.20 = f32[8,64,512]{2,1,0:T(8,128)S(1)} all-to-all(f32[8,64,512]{2,1,0:T(8,128)S(1)} %bitcast.93), channel_id=1, replica_groups=mesh['rows'=8,'pairs'=16] {'rows'}, dimensions={0} | all-to-all | bytes 2097152 | tf_op jit(solution)/shard_map/all_to_all | solution.py:53
  127.3 1.1 broadcast_in_dim.6
  128.4 3.6 %all-to-all-start.2 = ((f32[8,64,512]{2,1,0:T(8,128)}), f32[8,64,512]{2,1,0:T(8,128)S(1)}, u32[]{:S(2)}, u32[]{:S(2)}) async-start(f32[8,64,512]{2,1,0:T(8,128)} %broadcast_in_dim.6), calls=%async_computation.2 | async-start | bytes 2097152 | tf_op jit(solution)/shard_map/all_to_all | solution.py:56
  132.0 14.1 %all-to-all-done.2 = f32[8,64,512]{2,1,0:T(8,128)S(1)} async-done(((f32[8,64,512]{2,1,0:T(8,128)}), f32[8,64,512]{2,1,0:T(8,128)S(1)}, u32[]{:S(2)}, u32[]{:S(2)}) %all-to-all-start.2) | async-done | bytes 1048608 | tf_op jit(solution)/shard_map/all_to_all | solution.py:56
  146.6 0.4 copy-done.4
  147.0 1.9 convert_subtract_fusion.5
  149.7 1.1 fusion.24
  150.8 1.0 copy-done.9
  151.8 0.9 fusion.11
  152.7 1.6 copy.18
  154.3 24.3 %while.30 = (s32[]{:T(128)}, f32[512,512]{1,0:T(8,128)S(1)}, f32[512,512]{0,1:T(8,128)S(1)}, f32[]{:T(128)}, f32[512,512]{1,0:T(8,128)S(1)}, /*index=5*/s32[]{:T(128)}) while((s32[]{:T(128)}, f32[512,512]{1,0:T(8,128)S(1)}, f32[512,512]{0,1:T(8,128)S(1)}, f32[]{:T(128)}, f32[512,512]{1,0:T(8,128)S(1)}, /*index=5*/s32[]{:T(128)}) %tuple.58), condition=%wide.region_9.10_spmd.clone, body=%wide.region_7.9_spmd.clone.sunk | while | flops 2417491968 | bytes 8388693 | solution.py:46
  155.2 1.0 convolution_add_fusion.7
  156.2 4.1 %multiply_reduce_fusion.6 = (f32[]{:T(128)}, f32[512,512]{0,1:T(8,128)S(1)}) fusion(f32[512,512]{1,0:T(8,128)S(1)} %convolution_add_fusion.7, f32[512,512]{1,0:T(8,128)S(1)} %get-tuple-element.253), kind=kOutput, calls=%fused_computation.7.clone.1 | convolution fusion | flops 1611923456 | bytes 3145732 | tf_op jit(solution)/shard_map/while/body/dot_general | solution.py:42
  161.0 1.0 convolution_add_fusion.7
  162.1 4.1 %multiply_reduce_fusion.6 = (f32[]{:T(128)}, f32[512,512]{0,1:T(8,128)S(1)}) fusion(f32[512,512]{1,0:T(8,128)S(1)} %convolution_add_fusion.7, f32[512,512]{1,0:T(8,128)S(1)} %get-tuple-element.253), kind=kOutput, calls=%fused_computation.7.clone.1 | convolution fusion | flops 1611923456 | bytes 3145732 | tf_op jit(solution)/shard_map/while/body/dot_general | solution.py:42
  166.9 1.0 convolution_add_fusion.7
  168.0 4.1 %multiply_reduce_fusion.6 = (f32[]{:T(128)}, f32[512,512]{0,1:T(8,128)S(1)}) fusion(f32[512,512]{1,0:T(8,128)S(1)} %convolution_add_fusion.7, f32[512,512]{1,0:T(8,128)S(1)} %get-tuple-element.253), kind=kOutput, calls=%fused_computation.7.clone.1 | convolution fusion | flops 1611923456 | bytes 3145732 | tf_op jit(solution)/shard_map/while/body/dot_general | solution.py:42
  172.8 1.0 convolution_add_fusion.7
  173.8 4.1 %multiply_reduce_fusion.6 = (f32[]{:T(128)}, f32[512,512]{0,1:T(8,128)S(1)}) fusion(f32[512,512]{1,0:T(8,128)S(1)} %convolution_add_fusion.7, f32[512,512]{1,0:T(8,128)S(1)} %get-tuple-element.253), kind=kOutput, calls=%fused_computation.7.clone.1 | convolution fusion | flops 1611923456 | bytes 3145732 | tf_op jit(solution)/shard_map/while/body/dot_general | solution.py:42
  178.6 1.1 convolution_add_fusion.4
  179.8 0.3 copy-done.8
  180.1 2.1 fusion.7
  182.3 1.8 fusion.48
  184.1 1.7 fusion.46
  185.8 3.8 %collective-permute-start = (f32[1024,256]{1,0:T(8,128)}, f32[1024,256]{1,0:T(8,128)}, u32[]{:S(2)}, u32[]{:S(2)}) collective-permute-start(f32[1024,256]{1,0:T(8,128)} %get-tuple-element.156), channel_id=1, source_target_pairs={{0,1},{1,2},{2,3},{3,4},{4,5},{5,6},{6,7},{7,8},{8,9},{9,10},{10,1... | collective-permute-start | bytes 3145736 | tf_op jit(solution)/shard_map/ppermute | solution.py:22
  189.6 2.4 collective-permute-start.2
  192.0 9.6 %collective-permute-done = f32[1024,256]{1,0:T(8,128)} collective-permute-done((f32[1024,256]{1,0:T(8,128)}, f32[1024,256]{1,0:T(8,128)}, u32[]{:S(2)}, u32[]{:S(2)}) %collective-permute-start) | collective-permute-done | bytes 1048608 | tf_op jit(solution)/shard_map/ppermute | solution.py:22
  201.6 4.4 %collective-permute-done.2 = f32[1024,256]{1,0:T(8,128)} collective-permute-done((f32[1024,256]{1,0:T(8,128)}, f32[1024,256]{1,0:T(8,128)}, u32[]{:S(2)}, u32[]{:S(2)}) %collective-permute-start.2) | collective-permute-done | bytes 1048608 | tf_op jit(solution)/shard_map/ppermute | solution.py:22
  206.0 2.5 fusion.43
  208.6 1.5 broadcast_in_dim.7
  210.1 4.7 %all-to-all-start.3 = ((f32[8,256,256]{2,1,0:T(8,128)}), f32[8,256,256]{2,1,0:T(8,128)}, u32[]{:S(2)}, u32[]{:S(2)}) async-start(f32[8,256,256]{2,1,0:T(8,128)} %broadcast_in_dim.7), calls=%async_computation.3 | async-start | bytes 4194304 | tf_op jit(solution)/shard_map/all_to_all | solution.py:88
  214.8 1.0 fusion.49
  215.8 0.6 fusion.32
  216.5 0.6 broadcast_select_fusion.2
  217.1 1.9 collective-permute-start.1
  219.0 2.4 collective-permute-start.3
  221.4 0.9 collective-permute-done.1
  222.3 4.8 %collective-permute-done.3 = f32[256,256]{1,0:T(8,128)S(1)} collective-permute-done((f32[256,256]{1,0:T(8,128)S(1)}, f32[256,256]{1,0:T(8,128)S(1)}, u32[]{:S(2)}, u32[]{:S(2)}) %collective-permute-start.3) | collective-permute-done | bytes 262176 | tf_op jit(solution)/shard_map/ppermute | solution.py:22
  227.1 18.9 %all-to-all-done.3 = f32[8,256,256]{2,1,0:T(8,128)} async-done(((f32[8,256,256]{2,1,0:T(8,128)}), f32[8,256,256]{2,1,0:T(8,128)}, u32[]{:S(2)}, u32[]{:S(2)}) %all-to-all-start.3) | async-done | bytes 2097184 | tf_op jit(solution)/shard_map/all_to_all | solution.py:88
  246.1 1.8 reduce_sum.117
  248.0 2.2 convert_subtract_fusion.2
  251.2 2.1 fusion.25
  253.3 1.6 copy.23
  254.9 2.1 multiply_reduce_fusion.2
  257.0 29.8 %while.31 = (s32[]{:T(128)}, f32[512,512]{1,0:T(8,128)S(1)}, f32[512,512]{0,1:T(8,128)S(1)}, f32[]{:T(128)}, f32[512,512]{1,0:T(8,128)S(1)}, /*index=5*/s32[]{:T(128)}) while((s32[]{:T(128)}, f32[512,512]{1,0:T(8,128)S(1)}, f32[512,512]{0,1:T(8,128)S(1)}, f32[]{:T(128)}, f32[512,512]{1,0:T(8,128)S(1)}, ...), condition=%wide.region_16.17_spmd.clone, body=%wide.region_14.16_spmd.clone.sunk | while | flops 2417491968 | bytes 8388693 | solution.py:46
  257.6 1.0 convolution_add_fusion.8
  258.6 4.1 %multiply_reduce_fusion.7 = (f32[]{:T(128)}, f32[512,512]{0,1:T(8,128)S(1)}) fusion(f32[512,512]{1,0:T(8,128)S(1)} %convolution_add_fusion.8, f32[512,512]{1,0:T(8,128)S(1)} %get-tuple-element.271), kind=kOutput, calls=%fused_computation.12.clone.1 | convolution fusion | flops 1611923456 | bytes 3145732 | tf_op jit(solution)/shard_map/while/body/dot_general | solution.py:42
  263.4 1.0 convolution_add_fusion.8
  264.4 4.1 %multiply_reduce_fusion.7 = (f32[]{:T(128)}, f32[512,512]{0,1:T(8,128)S(1)}) fusion(f32[512,512]{1,0:T(8,128)S(1)} %convolution_add_fusion.8, f32[512,512]{1,0:T(8,128)S(1)} %get-tuple-element.271), kind=kOutput, calls=%fused_computation.12.clone.1 | convolution fusion | flops 1611923456 | bytes 3145732 | tf_op jit(solution)/shard_map/while/body/dot_general | solution.py:42
  269.2 1.0 convolution_add_fusion.8
  270.2 4.1 %multiply_reduce_fusion.7 = (f32[]{:T(128)}, f32[512,512]{0,1:T(8,128)S(1)}) fusion(f32[512,512]{1,0:T(8,128)S(1)} %convolution_add_fusion.8, f32[512,512]{1,0:T(8,128)S(1)} %get-tuple-element.271), kind=kOutput, calls=%fused_computation.12.clone.1 | convolution fusion | flops 1611923456 | bytes 3145732 | tf_op jit(solution)/shard_map/while/body/dot_general | solution.py:42
  275.0 1.0 convolution_add_fusion.8
  276.0 4.1 %multiply_reduce_fusion.7 = (f32[]{:T(128)}, f32[512,512]{0,1:T(8,128)S(1)}) fusion(f32[512,512]{1,0:T(8,128)S(1)} %convolution_add_fusion.8, f32[512,512]{1,0:T(8,128)S(1)} %get-tuple-element.271), kind=kOutput, calls=%fused_computation.12.clone.1 | convolution fusion | flops 1611923456 | bytes 3145732 | tf_op jit(solution)/shard_map/while/body/dot_general | solution.py:42
  280.8 1.0 convolution_add_fusion.8
  281.8 4.1 %multiply_reduce_fusion.7 = (f32[]{:T(128)}, f32[512,512]{0,1:T(8,128)S(1)}) fusion(f32[512,512]{1,0:T(8,128)S(1)} %convolution_add_fusion.8, f32[512,512]{1,0:T(8,128)S(1)} %get-tuple-element.271), kind=kOutput, calls=%fused_computation.12.clone.1 | convolution fusion | flops 1611923456 | bytes 3145732 | tf_op jit(solution)/shard_map/while/body/dot_general | solution.py:42
  286.8 1.1 convolution_add_fusion.3
  288.2 2.2 fusion.14
  290.4 2.3 fusion.26
  292.6 3.6 %convolution_add_fusion.2 = f32[1024,512]{1,0:T(8,128)} fusion(f32[1024,512]{1,0:T(8,128)S(1)} %fusion.26, f32[512,512]{1,0:T(8,128)S(1)} %fusion.14, f32[1024,256]{1,0:T(8,128)} %collective-permute-done, f32[1024,512]{1,0:T(8,128)S(1)} %copy-done.3, pred[]{:T(512)S(6)} %eq.39), kind=kOutput, calls=%fused_computation.23 | convolution fusion | flops 806092800 | bytes 6815745 | tf_op jit(solution)/shard_map/dot_general | solution.py:161
  (63 shorter events, 2.6 us)
Async XLA Ops:
  6.0 8.5 %copy-start.18 = (s32[1,16]{1,0:T(1,128)S(1)}, s32[1,16]{1,0:T(1,128)}, u32[]{:S(2)}) copy-start(s32[1,16]{1,0:T(1,128)} %param.9) | copy-start | bytes 196
  6.0 93.7 %all-to-all-start = ((f32[16,192,512]{2,1,0:T(8,128)}), f32[16,192,512]{2,1,0:T(8,128)}, u32[]{:S(2)}, u32[]{:S(2)}) async-start(f32[16,192,512]{2,1,0:T(8,128)} %shard_map.46), calls=%async_computation | async-start | bytes 12582912 | tf_op jit(solution)/shard_map/all_to_all | solution.py:180
  106.5 1.9 copy-start
  128.4 17.6 %all-to-all-start.2 = ((f32[8,64,512]{2,1,0:T(8,128)}), f32[8,64,512]{2,1,0:T(8,128)S(1)}, u32[]{:S(2)}, u32[]{:S(2)}) async-start(f32[8,64,512]{2,1,0:T(8,128)} %broadcast_in_dim.6), calls=%async_computation.2 | async-start | bytes 2097152 | tf_op jit(solution)/shard_map/all_to_all | solution.py:56
  146.0 1.0 copy-start.4
  148.9 1.9 copy-start.7
  150.8 1.0 copy-start.9
  178.6 1.2 copy-start.5
  178.6 1.5 copy-start.8
  180.1 2.2 copy-start.1
  184.1 21.9 %copy-start.2 = (f32[1024,512]{1,0:T(8,128)}, f32[1024,512]{1,0:T(8,128)S(1)}, u32[]{:S(2)}) copy-start(f32[1024,512]{1,0:T(8,128)S(1)} %fusion.48) | copy-start | bytes 6291460
  185.8 15.8 %collective-permute-start = (f32[1024,256]{1,0:T(8,128)}, f32[1024,256]{1,0:T(8,128)}, u32[]{:S(2)}, u32[]{:S(2)}) collective-permute-start(f32[1024,256]{1,0:T(8,128)} %get-tuple-element.156), channel_id=1, source_target_pairs={{0,1},{1,2},{2,3},{3,4},{4,5},{5,6},{6,7},{7,8},{8,9},{9,10},{10,1... | collective-permute-start | bytes 3145736 | tf_op jit(solution)/shard_map/ppermute | solution.py:22
  189.6 16.4 %collective-permute-start.2 = (f32[1024,256]{1,0:T(8,128)}, f32[1024,256]{1,0:T(8,128)}, u32[]{:S(2)}, u32[]{:S(2)}) collective-permute-start(f32[1024,256]{1,0:T(8,128)} %get-tuple-element.155), channel_id=1, source_target_pairs={{1,0},{2,1},{3,2},{4,3},{5,4},{6,5},{7,6},{8,7},{9,8},{10,9},{11,1... | collective-permute-start | bytes 3145736 | tf_op jit(solution)/shard_map/ppermute | solution.py:22
  210.1 4.7 %copy-start.6 = (f32[8,64,512]{2,1,0:T(8,128)S(1)}, f32[8,64,512]{2,1,0:T(8,128)}, u32[]{:S(2)}) copy-start(f32[8,64,512]{2,1,0:T(8,128)} %copy-done.4) | copy-start | bytes 3145732
  210.1 36.0 %all-to-all-start.3 = ((f32[8,256,256]{2,1,0:T(8,128)}), f32[8,256,256]{2,1,0:T(8,128)}, u32[]{:S(2)}, u32[]{:S(2)}) async-start(f32[8,256,256]{2,1,0:T(8,128)} %broadcast_in_dim.7), calls=%async_computation.3 | async-start | bytes 4194304 | tf_op jit(solution)/shard_map/all_to_all | solution.py:88
  217.1 5.2 %collective-permute-start.1 = (f32[256,256]{1,0:T(8,128)S(1)}, f32[256,256]{1,0:T(8,128)S(1)}, u32[]{:S(2)}, u32[]{:S(2)}) collective-permute-start(f32[256,256]{1,0:T(8,128)S(1)} %get-tuple-element.164), channel_id=1, source_target_pairs={{0,1},{1,2},{2,3},{3,4},{4,5},{5,6},{6,7},{7,8},{8,9},{9,10},{10,1... | collective-permute-start | bytes 786440 | tf_op jit(solution)/shard_map/ppermute | solution.py:22
  219.0 8.1 %collective-permute-start.3 = (f32[256,256]{1,0:T(8,128)S(1)}, f32[256,256]{1,0:T(8,128)S(1)}, u32[]{:S(2)}, u32[]{:S(2)}) collective-permute-start(f32[256,256]{1,0:T(8,128)S(1)} %get-tuple-element.165), channel_id=1, source_target_pairs={{1,0},{2,1},{3,2},{4,3},{5,4},{6,5},{7,6},{8,7},{9,8},{10,9},{11,1... | collective-permute-start | bytes 786440 | tf_op jit(solution)/shard_map/ppermute | solution.py:22
  227.1 23.1 %copy-start.14 = (f32[256,256]{1,0:T(8,128)}, f32[256,256]{1,0:T(8,128)S(1)}, u32[]{:S(2)}) copy-start(f32[256,256]{1,0:T(8,128)S(1)} %get-tuple-element.161) | copy-start | bytes 786436
  227.1 23.1 %copy-start.16 = (f32[256,256]{1,0:T(8,128)}, f32[256,256]{1,0:T(8,128)S(1)}, u32[]{:S(2)}) copy-start(f32[256,256]{1,0:T(8,128)S(1)} %get-tuple-element.162) | copy-start | bytes 786436
  248.0 2.3 copy-start.12
  250.2 1.0 copy-start.10
  286.8 1.2 copy-start.11
  286.8 1.3 copy-start.13
  286.8 1.3 copy-start.15
  286.8 1.4 copy-start.17
  288.2 2.2 copy-start.3

commit v2 on v1

--- a/solution.py
+++ b/solution.py
@@ -112,19 +112,22 @@
     )
     gram_full = row_sum(partial_gram, "rows")
     rotation = cayley(gram_full)
-    turned = jnp.dot(panels, rotation, precision=BIG)
+    half_width = panels.shape[1] // 2
+    turned_lower = jnp.dot(panels, rotation[:, half_width:], precision=BIG)
+    turned_upper = jnp.dot(panels, rotation[:, :half_width], precision=BIG)
     gram_turned = jnp.dot(gram_full, rotation, precision=BIG)
-    half_width = panels.shape[1] // 2
     block_gram = lambda cut: lax.dot_general(
         rotation[:, cut], gram_turned[:, cut], (((0,), (0,)), ((), ())), precision=BIG
     )
-    return turned, block_gram(slice(0, half_width)), block_gram(slice(half_width, None))
+    return (
+        turned_upper,
+        turned_lower,
+        block_gram(slice(0, half_width)),
+        block_gram(slice(half_width, None)),
+    )
 
 
-def advance(panels, upper_gram, lower_gram):
-    half_width = panels.shape[1] // 2
-    upper = panels[:, :half_width]
-    lower = panels[:, half_width:]
+def advance(upper, lower, upper_gram, lower_gram):
     pair_index = lax.axis_index("pairs")
     last_pair = lax.axis_size("pairs") - 1
     first = pair_index == 0

time: 297 us -> 309 us (1.040)
  matrix products: 74.3 us -> 80.9 us
  local copies, waits for them, and re-layouts: 15.7 us -> 21.4 us
    while x9 -> x35, local copies, waits for them, and re-layouts: 0.63 us -> 6.06 us
    dot_general x9, matrix products: 37 us -> 41.1 us  [body(): residual = identity - jnp.dot(sym_part, inverse, precision=HI)]
where the time goes in v2:
time: 309 us; the launch traced here: 307 us
  waiting for transfers between devices  137 us (44%)
  matrix products  80.9 us (26%)
  starting transfers between devices  27.3 us (9%)
  local copies, waits for them, and re-layouts  21.4 us (7%)
  blocking collectives  18.8 us (6%)
  loops' own time  7.6 us (2%)
  Pallas kernels  6.04 us (2%)
  other arithmetic  5.94 us (2%)
    all_to_all x1, waiting for transfers between devices, local(): panels = lax.all_to_all(seated, 'pairs', 0, 0, tiled=True)  84.8 us
    dot_general x9, matrix products, body(): residual = identity - jnp.dot(sym_part, inverse, precision=HI)  41.1 us
    ppermute x4, waiting for transfers between devices, passed_along(): return lax.ppermute(array, axis, pairs)  19.6 us
    all_to_all x1, blocking collectives, row_sum(): lax.all_to_all(partial.reshape(count, rows // count, cols), axis, 0, 0, t...  18.8 us
    all_to_all x1, waiting for transfers between devices, row_gather_sum(): return jnp.sum(lax.all_to_all(spread, axis, 0, 0, tiled=False), axis=0)  18.7 us
    all_to_all x1, waiting for transfers between devices, row_sum(): return lax.all_to_all(spread, axis, 0, 0, tiled=False).reshape(rows, cols)  14.1 us
    ppermute x4, starting transfers between devices, passed_along(): return lax.ppermute(array, axis, pairs)  10.5 us
    dot_general x9, matrix products, body(): inverse = inverse + jnp.dot(inverse, residual, precision=BIG)  9.28 us
  transfers between devices with their start and end apart: 7, of which 7 were waited for; matrix products, arithmetic and copies ran while one was open for 1% of the time, Pallas kernels for 0%

profile of v2, /device:TPU:3, one launch (start us, length us, event | category | flops | bytes accessed | tf_op | source)
XLA Modules:
  0.0 306.9 jit_solution(2695859941301909181)
XLA Ops:
  0.0 6.0 %shard_map.46 = f32[16,192,512]{2,1,0:T(8,128)} custom-call(s32[32]{0:T(128)} %seat_ref.1, f32[192,8192]{1,0:T(8,128)} %bitcast.58, f32[192,8192]{1,0:T(8,128)} %bitcast.59, f32[192,8192]{1,0:T(8,128)} %bitcast.60, f32[192,8192]{1,0:T(8,128)} %bitcast.61, f32[192,8192]{1,0:T(8,128)} %bitcast.62, f32[192,8192]{1,0:T(8,128)} %bitcast.63, ...), custom_call_target="tpu_custom_call" | custom-call | tf_op jit(solution)/shard_map/pallas_call | solution.py:72
  6.1 8.5 %all-to-all-start = ((f32[16,192,512]{2,1,0:T(8,128)}), f32[16,192,512]{2,1,0:T(8,128)}, u32[]{:S(2)}, u32[]{:S(2)}) async-start(f32[16,192,512]{2,1,0:T(8,128)} %shard_map.46), calls=%async_computation | async-start | bytes 12582912 | tf_op jit(solution)/shard_map/all_to_all | solution.py:183
  14.9 84.8 %all-to-all-done = f32[16,192,512]{2,1,0:T(8,128)} async-done(((f32[16,192,512]{2,1,0:T(8,128)}), f32[16,192,512]{2,1,0:T(8,128)}, u32[]{:S(2)}, u32[]{:S(2)}) %all-to-all-start) | async-done | bytes 6291488 | tf_op jit(solution)/shard_map/all_to_all | solution.py:183
  99.7 6.8 %gather_fusion = f32[1024,512]{1,0:T(8,128)S(1)} fusion(f32[3072,512]{1,0:T(8,128)} %bitcast.2, s32[1024]{0:T(1024)S(1)} %broadcast_clamp_fusion), kind=kCustom, calls=%fused_computation | custom fusion | bytes 4198400 | tf_op jit(solution)/shard_map/jit(_take)/gather | solution.py:176
  106.5 1.8 fusion.50
  108.4 18.8 %all_to_all.20 = f32[8,64,512]{2,1,0:T(8,128)S(1)} all-to-all(f32[8,64,512]{2,1,0:T(8,128)S(1)} %bitcast.93), channel_id=1, replica_groups=mesh['rows'=8,'pairs'=16] {'rows'}, dimensions={0} | all-to-all | bytes 2097152 | tf_op jit(solution)/shard_map/all_to_all | solution.py:53
  127.2 1.1 broadcast_in_dim.6
  128.3 3.6 %all-to-all-start.2 = ((f32[8,64,512]{2,1,0:T(8,128)}), f32[8,64,512]{2,1,0:T(8,128)S(1)}, u32[]{:S(2)}, u32[]{:S(2)}) async-start(f32[8,64,512]{2,1,0:T(8,128)} %broadcast_in_dim.6), calls=%async_computation.2 | async-start | bytes 2097152 | tf_op jit(solution)/shard_map/all_to_all | solution.py:56
  131.9 14.1 %all-to-all-done.2 = f32[8,64,512]{2,1,0:T(8,128)S(1)} async-done(((f32[8,64,512]{2,1,0:T(8,128)}), f32[8,64,512]{2,1,0:T(8,128)S(1)}, u32[]{:S(2)}, u32[]{:S(2)}) %all-to-all-start.2) | async-done | bytes 1048608 | tf_op jit(solution)/shard_map/all_to_all | solution.py:56
  146.6 2.9 convert_subtract_fusion.5
  150.2 2.7 fusion.24
  152.9 1.0 copy-done.14
  153.9 0.9 fusion.11
  154.9 2.6 copy.18
  157.4 33.5 %while.30 = (s32[]{:T(128)}, f32[512,512]{1,0:T(8,128)S(1)}, f32[512,512]{0,1:T(8,128)}, f32[]{:T(128)}, f32[512,512]{1,0:T(8,128)}, /*index=5*/s32[]{:T(128)}) while((s32[]{:T(128)}, f32[512,512]{1,0:T(8,128)S(1)}, f32[512,512]{0,1:T(8,128)}, f32[]{:T(128)}, f32[512,512]{1,0:T(8,128)}, /*index=5*/s32[]{:T(128)}) %tuple.58), condition=%wide.region_9.10_spmd.clone, body=%wide.region_7.9_spmd.clone.sunk | while | flops 2417491968 | bytes 16777356 | solution.py:46
  158.4 1.1 copy-done
  159.5 1.0 convolution_add_fusion.7
  160.6 5.2 %multiply_reduce_fusion.6 = (f32[]{:T(128)}, f32[512,512]{0,1:T(8,128)}) fusion(f32[512,512]{1,0:T(8,128)S(1)} %convolution_add_fusion.7, f32[512,512]{1,0:T(8,128)S(1)} %copy-done.1), kind=kOutput, calls=%fused_computation.7.clone.1 | convolution fusion | flops 1611923456 | bytes 3145732 | tf_op jit(solution)/shard_map/while/body/dot_general | solution.py:42
  166.6 1.1 copy-done
  167.7 1.0 convolution_add_fusion.7
  168.7 5.2 %multiply_reduce_fusion.6 = (f32[]{:T(128)}, f32[512,512]{0,1:T(8,128)}) fusion(f32[512,512]{1,0:T(8,128)S(1)} %convolution_add_fusion.7, f32[512,512]{1,0:T(8,128)S(1)} %copy-done.1), kind=kOutput, calls=%fused_computation.7.clone.1 | convolution fusion | flops 1611923456 | bytes 3145732 | tf_op jit(solution)/shard_map/while/body/dot_general | solution.py:42
  174.7 1.1 copy-done
  175.8 1.0 convolution_add_fusion.7
  176.9 5.2 %multiply_reduce_fusion.6 = (f32[]{:T(128)}, f32[512,512]{0,1:T(8,128)}) fusion(f32[512,512]{1,0:T(8,128)S(1)} %convolution_add_fusion.7, f32[512,512]{1,0:T(8,128)S(1)} %copy-done.1), kind=kOutput, calls=%fused_computation.7.clone.1 | convolution fusion | flops 1611923456 | bytes 3145732 | tf_op jit(solution)/shard_map/while/body/dot_general | solution.py:42
  182.9 1.1 copy-done
  184.0 1.0 convolution_add_fusion.7
  185.0 5.2 %multiply_reduce_fusion.6 = (f32[]{:T(128)}, f32[512,512]{0,1:T(8,128)}) fusion(f32[512,512]{1,0:T(8,128)S(1)} %convolution_add_fusion.7, f32[512,512]{1,0:T(8,128)S(1)} %copy-done.1), kind=kOutput, calls=%fused_computation.7.clone.1 | convolution fusion | flops 1611923456 | bytes 3145732 | tf_op jit(solution)/shard_map/while/body/dot_general | solution.py:42
  190.9 2.5 convolution_add_fusion.4
  193.4 2.2 fusion.7
  195.6 1.0 fusion.45
  196.6 2.3 broadcast_select_fusion.2
  198.9 3.8 %collective-permute-start = (f32[1024,256]{1,0:T(8,128)}, f32[1024,256]{1,0:T(8,128)S(1)}, u32[]{:S(2)}, u32[]{:S(2)}) collective-permute-start(f32[1024,256]{1,0:T(8,128)} %get-tuple-element.164), channel_id=1, source_target_pairs={{0,1},{1,2},{2,3},{3,4},{4,5},{5,6},{6,7},{7,8},{8,9},{9,10},{10,1... | collective-permute-start | bytes 3145736 | tf_op jit(solution)/shard_map/ppermute | solution.py:22
  202.7 2.4 collective-permute-start.2
  205.1 9.6 %collective-permute-done = f32[1024,256]{1,0:T(8,128)S(1)} collective-permute-done((f32[1024,256]{1,0:T(8,128)}, f32[1024,256]{1,0:T(8,128)S(1)}, u32[]{:S(2)}, u32[]{:S(2)}) %collective-permute-start) | collective-permute-done | bytes 1048608 | tf_op jit(solution)/shard_map/ppermute | solution.py:22
  214.7 4.3 %collective-permute-done.2 = f32[1024,256]{1,0:T(8,128)S(1)} collective-permute-done((f32[1024,256]{1,0:T(8,128)}, f32[1024,256]{1,0:T(8,128)S(1)}, u32[]{:S(2)}, u32[]{:S(2)}) %collective-permute-start.2) | collective-permute-done | bytes 1048608 | tf_op jit(solution)/shard_map/ppermute | solution.py:22
  219.0 1.0 fusion.47
  220.1 1.5 broadcast_in_dim.7
  221.6 4.7 %all-to-all-start.3 = ((f32[8,256,256]{2,1,0:T(8,128)}), f32[8,256,256]{2,1,0:T(8,128)}, u32[]{:S(2)}, u32[]{:S(2)}) async-start(f32[8,256,256]{2,1,0:T(8,128)} %broadcast_in_dim.7), calls=%async_computation.3 | async-start | bytes 4194304 | tf_op jit(solution)/shard_map/all_to_all | solution.py:88
  226.3 1.0 fusion.51
  228.5 1.9 collective-permute-start.1
  230.4 2.4 collective-permute-start.3
  232.8 0.9 collective-permute-done.1
  233.7 4.8 %collective-permute-done.3 = f32[256,256]{1,0:T(8,128)S(1)} collective-permute-done((f32[256,256]{1,0:T(8,128)S(1)}, f32[256,256]{1,0:T(8,128)S(1)}, u32[]{:S(2)}, u32[]{:S(2)}) %collective-permute-start.3) | collective-permute-done | bytes 262176 | tf_op jit(solution)/shard_map/ppermute | solution.py:22
  238.6 18.7 %all-to-all-done.3 = f32[8,256,256]{2,1,0:T(8,128)} async-done(((f32[8,256,256]{2,1,0:T(8,128)}), f32[8,256,256]{2,1,0:T(8,128)}, u32[]{:S(2)}, u32[]{:S(2)}) %all-to-all-start.3) | async-done | bytes 2097184 | tf_op jit(solution)/shard_map/all_to_all | solution.py:88
  257.3 1.8 reduce_sum.117
  259.3 3.1 %convert_subtract_fusion.2 = (f32[512,512]{1,0:T(8,128)}, f32[]{:T(128)}, f32[512,512]{1,0:T(8,128)S(1)}) fusion(f32[256,256]{1,0:T(8,128)S(1)} %get-tuple-element.160, f32[256,256]{1,0:T(8,128)S(1)} %bitcast.95, f32[256,256]{1,0:T(8,128)S(1)} %reduce_sum.117, f32[256,256]{1,0:T(8,128)S(1)} %get-tuple-element.159, f32[512]{0:T(512)S(1)} %integer_pow.40, ...), kind=kOutput, calls=%fused_computation.15 | convolution fusion | flops 809500672 | bytes 3149828 | tf_op jit(solution)/shard_map/dot_general | solution.py:99
  263.4 2.1 fusion.25
  265.5 1.6 copy.23
  267.0 2.1 multiply_reduce_fusion.2
  269.1 30.5 %while.31 = (s32[]{:T(128)}, f32[512,512]{1,0:T(8,128)S(1)}, f32[512,512]{0,1:T(8,128)S(1)}, f32[]{:T(128)}, f32[512,512]{1,0:T(8,128)}, /*index=5*/s32[]{:T(128)}) while((s32[]{:T(128)}, f32[512,512]{1,0:T(8,128)S(1)}, f32[512,512]{0,1:T(8,128)S(1)}, f32[]{:T(128)}, f32[512,512]{1,0:T(8,128)}, /*index=5*/s32[]{:T(128)}) %tuple.61), condition=%wide.region_16.17_spmd.clone, body=%wide.region_14.16_spmd.clone.sunk | while | flops 2417491968 | bytes 12583025 | solution.py:46
  269.8 1.0 convolution_add_fusion.8
  271.0 4.1 %multiply_reduce_fusion.7 = (f32[]{:T(128)}, f32[512,512]{0,1:T(8,128)S(1)}) fusion(f32[512,512]{1,0:T(8,128)S(1)} %convolution_add_fusion.8, f32[512,512]{1,0:T(8,128)S(1)} %copy-done.2), kind=kOutput, calls=%fused_computation.12.clone.1 | convolution fusion | flops 1611923456 | bytes 3145732 | tf_op jit(solution)/shard_map/while/body/dot_general | solution.py:42
  275.7 1.0 convolution_add_fusion.8
  276.9 4.1 %multiply_reduce_fusion.7 = (f32[]{:T(128)}, f32[512,512]{0,1:T(8,128)S(1)}) fusion(f32[512,512]{1,0:T(8,128)S(1)} %convolution_add_fusion.8, f32[512,512]{1,0:T(8,128)S(1)} %copy-done.2), kind=kOutput, calls=%fused_computation.12.clone.1 | convolution fusion | flops 1611923456 | bytes 3145732 | tf_op jit(solution)/shard_map/while/body/dot_general | solution.py:42
  281.7 1.0 convolution_add_fusion.8
  282.9 4.1 %multiply_reduce_fusion.7 = (f32[]{:T(128)}, f32[512,512]{0,1:T(8,128)S(1)}) fusion(f32[512,512]{1,0:T(8,128)S(1)} %convolution_add_fusion.8, f32[512,512]{1,0:T(8,128)S(1)} %copy-done.2), kind=kOutput, calls=%fused_computation.12.clone.1 | convolution fusion | flops 1611923456 | bytes 3145732 | tf_op jit(solution)/shard_map/while/body/dot_general | solution.py:42
  287.6 1.0 convolution_add_fusion.8
  288.8 4.1 %multiply_reduce_fusion.7 = (f32[]{:T(128)}, f32[512,512]{0,1:T(8,128)S(1)}) fusion(f32[512,512]{1,0:T(8,128)S(1)} %convolution_add_fusion.8, f32[512,512]{1,0:T(8,128)S(1)} %copy-done.2), kind=kOutput, calls=%fused_computation.12.clone.1 | convolution fusion | flops 1611923456 | bytes 3145732 | tf_op jit(solution)/shard_map/while/body/dot_general | solution.py:42
  293.5 1.0 convolution_add_fusion.8
  294.8 4.1 %multiply_reduce_fusion.7 = (f32[]{:T(128)}, f32[512,512]{0,1:T(8,128)S(1)}) fusion(f32[512,512]{1,0:T(8,128)S(1)} %convolution_add_fusion.8, f32[512,512]{1,0:T(8,128)S(1)} %copy-done.2), kind=kOutput, calls=%fused_computation.12.clone.1 | convolution fusion | flops 1611923456 | bytes 3145732 | tf_op jit(solution)/shard_map/while/body/dot_general | solution.py:42
  299.7 1.1 convolution_add_fusion.3
  301.1 2.2 fusion.14
  303.3 1.0 fusion.26
  304.5 2.4 convolution_add_fusion.2
  (93 shorter events, 4.8 us)
Async XLA Ops:
  6.0 8.5 %copy-start.23 = (s32[1,16]{1,0:T(1,128)S(1)}, s32[1,16]{1,0:T(1,128)}, u32[]{:S(2)}) copy-start(s32[1,16]{1,0:T(1,128)} %param.9) | copy-start | bytes 196
  6.1 93.7 %all-to-all-start = ((f32[16,192,512]{2,1,0:T(8,128)}), f32[16,192,512]{2,1,0:T(8,128)}, u32[]{:S(2)}, u32[]{:S(2)}) async-start(f32[16,192,512]{2,1,0:T(8,128)} %shard_map.46), calls=%async_computation | async-start | bytes 12582912 | tf_op jit(solution)/shard_map/all_to_all | solution.py:183
  128.3 17.6 %all-to-all-start.2 = ((f32[8,64,512]{2,1,0:T(8,128)}), f32[8,64,512]{2,1,0:T(8,128)S(1)}, u32[]{:S(2)}, u32[]{:S(2)}) async-start(f32[8,64,512]{2,1,0:T(8,128)} %broadcast_in_dim.6), calls=%async_computation.2 | async-start | bytes 2097152 | tf_op jit(solution)/shard_map/all_to_all | solution.py:56
  146.0 3.5 %copy-start.3 = (f32[8,64,512]{2,1,0:T(8,128)}, f32[8,64,512]{2,1,0:T(8,128)S(1)}, u32[]{:S(2)}) copy-start(f32[8,64,512]{2,1,0:T(8,128)S(1)} %all-to-all-done.2) | copy-start | bytes 3145732
  150.2 3.7 %copy-start.10 = (f32[512,512]{1,0:T(8,128)S(1)}, f32[512,512]{1,0:T(8,128)}, u32[]{:S(2)}) copy-start(f32[512,512]{1,0:T(8,128)} %get-tuple-element.161) | copy-start | bytes 3145732
  152.9 1.0 copy-start.14
  158.3 1.2 copy-start
  158.4 2.2 copy-start.1
  166.5 1.2 copy-start
  166.5 2.2 copy-start.1
  174.6 1.2 copy-start
  174.7 2.2 copy-start.1
  182.8 1.2 copy-start
  182.9 2.2 copy-start.1
  190.9 2.5 copy-start.4
  190.9 2.5 copy-start.11
  195.6 3.3 %copy-start.6 = (f32[512,512]{1,0:T(8,128)}, f32[512,512]{1,0:T(8,128)S(1)}, u32[]{:S(2)}) copy-start(f32[512,512]{1,0:T(8,128)S(1)} %fusion.7) | copy-start | bytes 3145732
  198.9 15.8 %collective-permute-start = (f32[1024,256]{1,0:T(8,128)}, f32[1024,256]{1,0:T(8,128)S(1)}, u32[]{:S(2)}, u32[]{:S(2)}) collective-permute-start(f32[1024,256]{1,0:T(8,128)} %get-tuple-element.164), channel_id=1, source_target_pairs={{0,1},{1,2},{2,3},{3,4},{4,5},{5,6},{6,7},{7,8},{8,9},{9,10},{10,1... | collective-permute-start | bytes 3145736 | tf_op jit(solution)/shard_map/ppermute | solution.py:22
  202.7 16.3 %collective-permute-start.2 = (f32[1024,256]{1,0:T(8,128)}, f32[1024,256]{1,0:T(8,128)S(1)}, u32[]{:S(2)}, u32[]{:S(2)}) collective-permute-start(f32[1024,256]{1,0:T(8,128)} %get-tuple-element.165), channel_id=1, source_target_pairs={{1,0},{2,1},{3,2},{4,3},{5,4},{6,5},{7,6},{8,7},{9,8},{10,9},{11,1... | collective-permute-start | bytes 3145736 | tf_op jit(solution)/shard_map/ppermute | solution.py:22
  214.7 5.3 %copy-start.12 = (f32[1024,256]{1,0:T(8,128)}, f32[1024,256]{1,0:T(8,128)S(1)}, u32[]{:S(2)}) copy-start(f32[1024,256]{1,0:T(8,128)S(1)} %collective-permute-done) | copy-start | bytes 3145732
  219.0 1.0 copy-start.8
  221.6 4.7 %copy-start.5 = (f32[8,64,512]{2,1,0:T(8,128)S(1)}, f32[8,64,512]{2,1,0:T(8,128)}, u32[]{:S(2)}) copy-start(f32[8,64,512]{2,1,0:T(8,128)} %copy-done.3) | copy-start | bytes 3145732
  221.6 4.7 %copy-start.7 = (f32[512,512]{1,0:T(8,128)S(1)}, f32[512,512]{1,0:T(8,128)}, u32[]{:S(2)}) copy-start(f32[512,512]{1,0:T(8,128)} %copy-done.6) | copy-start | bytes 3145732
  221.6 35.8 %all-to-all-start.3 = ((f32[8,256,256]{2,1,0:T(8,128)}), f32[8,256,256]{2,1,0:T(8,128)}, u32[]{:S(2)}, u32[]{:S(2)}) async-start(f32[8,256,256]{2,1,0:T(8,128)} %broadcast_in_dim.7), calls=%async_computation.3 | async-start | bytes 4194304 | tf_op jit(solution)/shard_map/all_to_all | solution.py:88
  228.5 5.2 %collective-permute-start.1 = (f32[256,256]{1,0:T(8,128)S(1)}, f32[256,256]{1,0:T(8,128)S(1)}, u32[]{:S(2)}, u32[]{:S(2)}) collective-permute-start(f32[256,256]{1,0:T(8,128)S(1)} %get-tuple-element.162), channel_id=1, source_target_pairs={{0,1},{1,2},{2,3},{3,4},{4,5},{5,6},{6,7},{7,8},{8,9},{9,10},{10,1... | collective-permute-start | bytes 786440 | tf_op jit(solution)/shard_map/ppermute | solution.py:22
  230.4 8.1 %collective-permute-start.3 = (f32[256,256]{1,0:T(8,128)S(1)}, f32[256,256]{1,0:T(8,128)S(1)}, u32[]{:S(2)}, u32[]{:S(2)}) collective-permute-start(f32[256,256]{1,0:T(8,128)S(1)} %get-tuple-element.163), channel_id=1, source_target_pairs={{1,0},{2,1},{3,2},{4,3},{5,4},{6,5},{7,6},{8,7},{9,8},{10,9},{11,1... | collective-permute-start | bytes 786440 | tf_op jit(solution)/shard_map/ppermute | solution.py:22
  238.6 23.8 %copy-start.19 = (f32[256,256]{1,0:T(8,128)}, f32[256,256]{1,0:T(8,128)S(1)}, u32[]{:S(2)}) copy-start(f32[256,256]{1,0:T(8,128)S(1)} %get-tuple-element.159) | copy-start | bytes 786436
  238.6 23.8 %copy-start.21 = (f32[256,256]{1,0:T(8,128)}, f32[256,256]{1,0:T(8,128)S(1)}, u32[]{:S(2)}) copy-start(f32[256,256]{1,0:T(8,128)S(1)} %get-tuple-element.160) | copy-start | bytes 786436
  259.2 3.2 %copy-start.17 = (f32[256,256]{0,1:T(8,128)}, f32[256,256]{0,1:T(8,128)S(1)}, u32[]{:S(2)}) copy-start(f32[256,256]{0,1:T(8,128)S(1)} %copy.21) | copy-start | bytes 786436
  262.4 1.0 copy-start.15
  269.8 1.2 copy-start.2
  275.7 1.2 copy-start.2
  281.6 1.2 copy-start.2
  287.6 1.2 copy-start.2
  293.5 1.2 copy-start.2
  299.7 1.2 copy-start.16
  299.7 1.3 copy-start.18
  299.7 1.3 copy-start.20
  299.7 1.4 copy-start.22
  301.1 2.2 copy-start.9
  303.3 1.2 copy-start.13

commit v3 on v1

--- a/solution.py
+++ b/solution.py
@@ -29,7 +29,7 @@
     scale = jnp.where(spread < 1.0, 1.0, 2.0 / (2.0 + spread))
     start = identity - scale * sym_part
     inverse = scale * (identity + start)
-    residual = lax.optimization_barrier(jnp.dot(start, start, precision=BIG))
+    residual = jnp.dot(start, start, precision=BIG)
     err = jnp.sum(residual * residual)
 
     def cond(state):

time: 297 us -> 296 us (level)
  no operation moved by 1% of the time
where the time goes in v3:
time: 296 us; the launch traced here: 295 us
  waiting for transfers between devices  137 us (46%)
  matrix products  76.5 us (26%)
  starting transfers between devices  27.3 us (9%)
  blocking collectives  18.8 us (6%)
  local copies, waits for them, and re-layouts  14.6 us (5%)
  loops' own time  7.18 us (2%)
  Pallas kernels  6.03 us (2%)
  other arithmetic  4.77 us (2%)
    all_to_all x1, waiting for transfers between devices, local(): panels = lax.all_to_all(seated, 'pairs', 0, 0, tiled=True)  84.8 us
    dot_general x9, matrix products, body(): residual = identity - jnp.dot(sym_part, inverse, precision=HI)  37 us
    ppermute x4, waiting for transfers between devices, passed_along(): return lax.ppermute(array, axis, pairs)  19.7 us
    all_to_all x1, waiting for transfers between devices, row_gather_sum(): return jnp.sum(lax.all_to_all(spread, axis, 0, 0, tiled=False), axis=0)  18.9 us
    all_to_all x1, blocking collectives, row_sum(): lax.all_to_all(partial.reshape(count, rows // count, cols), axis, 0, 0, t...  18.8 us
    all_to_all x1, waiting for transfers between devices, row_sum(): return lax.all_to_all(spread, axis, 0, 0, tiled=False).reshape(rows, cols)  14.1 us
    ppermute x4, starting transfers between devices, passed_along(): return lax.ppermute(array, axis, pairs)  10.5 us
    dot_general x9, matrix products, body(): inverse = inverse + jnp.dot(inverse, residual, precision=BIG)  9.28 us
  transfers between devices with their start and end apart: 7, of which 7 were waited for; matrix products, arithmetic and copies ran while one was open for 1% of the time, Pallas kernels for 0%

profile of v3, /device:TPU:3, one launch (start us, length us, event | category | flops | bytes accessed | tf_op | source)
XLA Modules:
  0.0 294.6 jit_solution(567583589584967187)
XLA Ops:
  0.0 6.0 %shard_map.46 = f32[16,192,512]{2,1,0:T(8,128)} custom-call(s32[32]{0:T(128)} %seat_ref.1, f32[192,8192]{1,0:T(8,128)} %bitcast.58, f32[192,8192]{1,0:T(8,128)} %bitcast.59, f32[192,8192]{1,0:T(8,128)} %bitcast.60, f32[192,8192]{1,0:T(8,128)} %bitcast.61, f32[192,8192]{1,0:T(8,128)} %bitcast.62, f32[192,8192]{1,0:T(8,128)} %bitcast.63, ...), custom_call_target="tpu_custom_call" | custom-call | tf_op jit(solution)/shard_map/pallas_call | solution.py:72
  6.0 8.5 %all-to-all-start = ((f32[16,192,512]{2,1,0:T(8,128)}), f32[16,192,512]{2,1,0:T(8,128)}, u32[]{:S(2)}, u32[]{:S(2)}) async-start(f32[16,192,512]{2,1,0:T(8,128)} %shard_map.46), calls=%async_computation | async-start | bytes 12582912 | tf_op jit(solution)/shard_map/all_to_all | solution.py:180
  14.9 84.8 %all-to-all-done = f32[16,192,512]{2,1,0:T(8,128)} async-done(((f32[16,192,512]{2,1,0:T(8,128)}), f32[16,192,512]{2,1,0:T(8,128)}, u32[]{:S(2)}, u32[]{:S(2)}) %all-to-all-start) | async-done | bytes 6291488 | tf_op jit(solution)/shard_map/all_to_all | solution.py:180
  99.7 6.8 %gather_fusion = f32[1024,512]{1,0:T(8,128)S(1)} fusion(f32[3072,512]{1,0:T(8,128)} %bitcast.2, s32[1024]{0:T(1024)S(1)} %broadcast_clamp_fusion), kind=kCustom, calls=%fused_computation | custom fusion | bytes 4198400 | tf_op jit(solution)/shard_map/jit(_take)/gather | solution.py:173
  106.5 1.8 fusion.47
  108.4 18.8 %all_to_all.20 = f32[8,64,512]{2,1,0:T(8,128)S(1)} all-to-all(f32[8,64,512]{2,1,0:T(8,128)S(1)} %bitcast.93), channel_id=1, replica_groups=mesh['rows'=8,'pairs'=16] {'rows'}, dimensions={0} | all-to-all | bytes 2097152 | tf_op jit(solution)/shard_map/all_to_all | solution.py:53
  127.3 1.1 broadcast_in_dim.6
  128.4 3.6 %all-to-all-start.2 = ((f32[8,64,512]{2,1,0:T(8,128)}), f32[8,64,512]{2,1,0:T(8,128)S(1)}, u32[]{:S(2)}, u32[]{:S(2)}) async-start(f32[8,64,512]{2,1,0:T(8,128)} %broadcast_in_dim.6), calls=%async_computation.2 | async-start | bytes 2097152 | tf_op jit(solution)/shard_map/all_to_all | solution.py:56
  132.0 14.1 %all-to-all-done.2 = f32[8,64,512]{2,1,0:T(8,128)S(1)} async-done(((f32[8,64,512]{2,1,0:T(8,128)}), f32[8,64,512]{2,1,0:T(8,128)S(1)}, u32[]{:S(2)}, u32[]{:S(2)}) %all-to-all-start.2) | async-done | bytes 1048608 | tf_op jit(solution)/shard_map/all_to_all | solution.py:56
  146.3 0.3 add_divide_fusion.1
  146.6 0.4 copy-done.4
  147.0 1.9 convert_subtract_fusion.5
  149.7 0.2 fusion.11
  149.9 2.8 multiply_reduce_fusion.3
  152.6 1.6 copy.18
  154.2 24.3 %while.30 = (s32[]{:T(128)}, f32[512,512]{1,0:T(8,128)S(1)}, f32[512,512]{0,1:T(8,128)S(1)}, f32[]{:T(128)}, f32[512,512]{1,0:T(8,128)S(1)}, /*index=5*/s32[]{:T(128)}) while((s32[]{:T(128)}, f32[512,512]{1,0:T(8,128)S(1)}, f32[512,512]{0,1:T(8,128)S(1)}, f32[]{:T(128)}, f32[512,512]{1,0:T(8,128)S(1)}, /*index=5*/s32[]{:T(128)}) %tuple.59), condition=%wide.region_9.10_spmd.clone, body=%wide.region_7.9_spmd.clone.sunk | while | flops 2417491968 | bytes 8388693 | solution.py:46
  155.1 1.0 convolution_add_fusion.7
  156.1 4.1 %multiply_reduce_fusion.6 = (f32[]{:T(128)}, f32[512,512]{0,1:T(8,128)S(1)}) fusion(f32[512,512]{1,0:T(8,128)S(1)} %convolution_add_fusion.7, f32[512,512]{1,0:T(8,128)S(1)} %get-tuple-element.255), kind=kOutput, calls=%fused_computation.7.clone.1 | convolution fusion | flops 1611923456 | bytes 3145732 | tf_op jit(solution)/shard_map/while/body/dot_general | solution.py:42
  161.0 1.0 convolution_add_fusion.7
  162.0 4.1 %multiply_reduce_fusion.6 = (f32[]{:T(128)}, f32[512,512]{0,1:T(8,128)S(1)}) fusion(f32[512,512]{1,0:T(8,128)S(1)} %convolution_add_fusion.7, f32[512,512]{1,0:T(8,128)S(1)} %get-tuple-element.255), kind=kOutput, calls=%fused_computation.7.clone.1 | convolution fusion | flops 1611923456 | bytes 3145732 | tf_op jit(solution)/shard_map/while/body/dot_general | solution.py:42
  166.8 1.0 convolution_add_fusion.7
  167.9 4.1 %multiply_reduce_fusion.6 = (f32[]{:T(128)}, f32[512,512]{0,1:T(8,128)S(1)}) fusion(f32[512,512]{1,0:T(8,128)S(1)} %convolution_add_fusion.7, f32[512,512]{1,0:T(8,128)S(1)} %get-tuple-element.255), kind=kOutput, calls=%fused_computation.7.clone.1 | convolution fusion | flops 1611923456 | bytes 3145732 | tf_op jit(solution)/shard_map/while/body/dot_general | solution.py:42
  172.7 1.0 convolution_add_fusion.7
  173.7 4.1 %multiply_reduce_fusion.6 = (f32[]{:T(128)}, f32[512,512]{0,1:T(8,128)S(1)}) fusion(f32[512,512]{1,0:T(8,128)S(1)} %convolution_add_fusion.7, f32[512,512]{1,0:T(8,128)S(1)} %get-tuple-element.255), kind=kOutput, calls=%fused_computation.7.clone.1 | convolution fusion | flops 1611923456 | bytes 3145732 | tf_op jit(solution)/shard_map/while/body/dot_general | solution.py:42
  178.5 1.1 convolution_add_fusion.4
  179.7 0.3 copy-done.8
  180.1 2.1 fusion.7
  182.2 1.8 fusion.48
  184.1 1.7 fusion.46
  185.7 3.8 %collective-permute-start = (f32[1024,256]{1,0:T(8,128)}, f32[1024,256]{1,0:T(8,128)}, u32[]{:S(2)}, u32[]{:S(2)}) collective-permute-start(f32[1024,256]{1,0:T(8,128)} %get-tuple-element.156), channel_id=1, source_target_pairs={{0,1},{1,2},{2,3},{3,4},{4,5},{5,6},{6,7},{7,8},{8,9},{9,10},{10,1... | collective-permute-start | bytes 3145736 | tf_op jit(solution)/shard_map/ppermute | solution.py:22
  189.5 2.4 collective-permute-start.2
  191.9 9.6 %collective-permute-done = f32[1024,256]{1,0:T(8,128)} collective-permute-done((f32[1024,256]{1,0:T(8,128)}, f32[1024,256]{1,0:T(8,128)}, u32[]{:S(2)}, u32[]{:S(2)}) %collective-permute-start) | collective-permute-done | bytes 1048608 | tf_op jit(solution)/shard_map/ppermute | solution.py:22
  201.5 4.4 %collective-permute-done.2 = f32[1024,256]{1,0:T(8,128)} collective-permute-done((f32[1024,256]{1,0:T(8,128)}, f32[1024,256]{1,0:T(8,128)}, u32[]{:S(2)}, u32[]{:S(2)}) %collective-permute-start.2) | collective-permute-done | bytes 1048608 | tf_op jit(solution)/shard_map/ppermute | solution.py:22
  205.9 2.5 fusion.43
  208.5 1.5 broadcast_in_dim.7
  210.0 4.7 %all-to-all-start.3 = ((f32[8,256,256]{2,1,0:T(8,128)}), f32[8,256,256]{2,1,0:T(8,128)}, u32[]{:S(2)}, u32[]{:S(2)}) async-start(f32[8,256,256]{2,1,0:T(8,128)} %broadcast_in_dim.7), calls=%async_computation.3 | async-start | bytes 4194304 | tf_op jit(solution)/shard_map/all_to_all | solution.py:88
  214.7 1.0 fusion.49
  215.8 0.6 fusion.32
  216.4 0.6 broadcast_select_fusion.2
  217.0 1.9 collective-permute-start.1
  218.9 2.4 collective-permute-start.3
  221.3 0.9 collective-permute-done.1
  222.2 4.8 %collective-permute-done.3 = f32[256,256]{1,0:T(8,128)S(1)} collective-permute-done((f32[256,256]{1,0:T(8,128)S(1)}, f32[256,256]{1,0:T(8,128)S(1)}, u32[]{:S(2)}, u32[]{:S(2)}) %collective-permute-start.3) | collective-permute-done | bytes 262176 | tf_op jit(solution)/shard_map/ppermute | solution.py:22
  227.1 18.9 %all-to-all-done.3 = f32[8,256,256]{2,1,0:T(8,128)} async-done(((f32[8,256,256]{2,1,0:T(8,128)}), f32[8,256,256]{2,1,0:T(8,128)}, u32[]{:S(2)}, u32[]{:S(2)}) %all-to-all-start.3) | async-done | bytes 2097184 | tf_op jit(solution)/shard_map/all_to_all | solution.py:88
  246.0 1.8 reduce_sum.117
  247.9 2.2 convert_subtract_fusion.2
  250.9 0.2 fusion.12
  251.1 2.7 multiply_reduce_fusion.2
  253.7 1.6 copy.23
  255.3 29.8 %while.31 = (s32[]{:T(128)}, f32[512,512]{1,0:T(8,128)S(1)}, f32[512,512]{0,1:T(8,128)S(1)}, f32[]{:T(128)}, f32[512,512]{1,0:T(8,128)S(1)}, /*index=5*/s32[]{:T(128)}) while((s32[]{:T(128)}, f32[512,512]{1,0:T(8,128)S(1)}, f32[512,512]{0,1:T(8,128)S(1)}, f32[]{:T(128)}, f32[512,512]{1,0:T(8,128)S(1)}, ...), condition=%wide.region_16.17_spmd.clone, body=%wide.region_14.16_spmd.clone.sunk | while | flops 2417491968 | bytes 8388693 | solution.py:46
  256.0 1.0 convolution_add_fusion.8
  257.0 4.1 %multiply_reduce_fusion.7 = (f32[]{:T(128)}, f32[512,512]{0,1:T(8,128)S(1)}) fusion(f32[512,512]{1,0:T(8,128)S(1)} %convolution_add_fusion.8, f32[512,512]{1,0:T(8,128)S(1)} %get-tuple-element.273), kind=kOutput, calls=%fused_computation.12.clone.1 | convolution fusion | flops 1611923456 | bytes 3145732 | tf_op jit(solution)/shard_map/while/body/dot_general | solution.py:42
  261.7 1.0 convolution_add_fusion.8
  262.8 4.1 %multiply_reduce_fusion.7 = (f32[]{:T(128)}, f32[512,512]{0,1:T(8,128)S(1)}) fusion(f32[512,512]{1,0:T(8,128)S(1)} %convolution_add_fusion.8, f32[512,512]{1,0:T(8,128)S(1)} %get-tuple-element.273), kind=kOutput, calls=%fused_computation.12.clone.1 | convolution fusion | flops 1611923456 | bytes 3145732 | tf_op jit(solution)/shard_map/while/body/dot_general | solution.py:42
  267.5 1.0 convolution_add_fusion.8
  268.6 4.1 %multiply_reduce_fusion.7 = (f32[]{:T(128)}, f32[512,512]{0,1:T(8,128)S(1)}) fusion(f32[512,512]{1,0:T(8,128)S(1)} %convolution_add_fusion.8, f32[512,512]{1,0:T(8,128)S(1)} %get-tuple-element.273), kind=kOutput, calls=%fused_computation.12.clone.1 | convolution fusion | flops 1611923456 | bytes 3145732 | tf_op jit(solution)/shard_map/while/body/dot_general | solution.py:42
  273.3 1.0 convolution_add_fusion.8
  274.4 4.1 %multiply_reduce_fusion.7 = (f32[]{:T(128)}, f32[512,512]{0,1:T(8,128)S(1)}) fusion(f32[512,512]{1,0:T(8,128)S(1)} %convolution_add_fusion.8, f32[512,512]{1,0:T(8,128)S(1)} %get-tuple-element.273), kind=kOutput, calls=%fused_computation.12.clone.1 | convolution fusion | flops 1611923456 | bytes 3145732 | tf_op jit(solution)/shard_map/while/body/dot_general | solution.py:42
  279.1 1.0 convolution_add_fusion.8
  280.2 4.1 %multiply_reduce_fusion.7 = (f32[]{:T(128)}, f32[512,512]{0,1:T(8,128)S(1)}) fusion(f32[512,512]{1,0:T(8,128)S(1)} %convolution_add_fusion.8, f32[512,512]{1,0:T(8,128)S(1)} %get-tuple-element.273), kind=kOutput, calls=%fused_computation.12.clone.1 | convolution fusion | flops 1611923456 | bytes 3145732 | tf_op jit(solution)/shard_map/while/body/dot_general | solution.py:42
  285.1 1.1 convolution_add_fusion.3
  286.5 2.2 fusion.14
  288.7 2.3 fusion.26
  291.0 3.6 %convolution_add_fusion.2 = f32[1024,512]{1,0:T(8,128)} fusion(f32[1024,512]{1,0:T(8,128)S(1)} %fusion.26, f32[512,512]{1,0:T(8,128)S(1)} %fusion.14, f32[1024,256]{1,0:T(8,128)} %collective-permute-done, f32[1024,512]{1,0:T(8,128)S(1)} %copy-done.3, pred[]{:T(512)S(6)} %eq.39), kind=kOutput, calls=%fused_computation.23 | convolution fusion | flops 806092800 | bytes 6815745 | tf_op jit(solution)/shard_map/dot_general | solution.py:161
  (60 shorter events, 2.0 us)
Async XLA Ops:
  6.0 8.5 %copy-start.17 = (s32[1,16]{1,0:T(1,128)S(1)}, s32[1,16]{1,0:T(1,128)}, u32[]{:S(2)}) copy-start(s32[1,16]{1,0:T(1,128)} %param.9) | copy-start | bytes 196
  6.0 93.7 %all-to-all-start = ((f32[16,192,512]{2,1,0:T(8,128)}), f32[16,192,512]{2,1,0:T(8,128)}, u32[]{:S(2)}, u32[]{:S(2)}) async-start(f32[16,192,512]{2,1,0:T(8,128)} %shard_map.46), calls=%async_computation | async-start | bytes 12582912 | tf_op jit(solution)/shard_map/all_to_all | solution.py:180
  106.5 1.9 copy-start
  128.4 17.6 %all-to-all-start.2 = ((f32[8,64,512]{2,1,0:T(8,128)}), f32[8,64,512]{2,1,0:T(8,128)S(1)}, u32[]{:S(2)}, u32[]{:S(2)}) async-start(f32[8,64,512]{2,1,0:T(8,128)} %broadcast_in_dim.6), calls=%async_computation.2 | async-start | bytes 2097152 | tf_op jit(solution)/shard_map/all_to_all | solution.py:56
  146.0 1.0 copy-start.4
  148.9 3.7 %copy-start.7 = (f32[512,512]{1,0:T(8,128)}, f32[512,512]{1,0:T(8,128)S(1)}, u32[]{:S(2)}) copy-start(f32[512,512]{1,0:T(8,128)S(1)} %get-tuple-element.163) | copy-start | bytes 3145732
  178.5 1.2 copy-start.5
  178.5 1.5 copy-start.8
  180.1 2.2 copy-start.1
  184.0 21.9 %copy-start.2 = (f32[1024,512]{1,0:T(8,128)}, f32[1024,512]{1,0:T(8,128)S(1)}, u32[]{:S(2)}) copy-start(f32[1024,512]{1,0:T(8,128)S(1)} %fusion.48) | copy-start | bytes 6291460
  185.7 15.8 %collective-permute-start = (f32[1024,256]{1,0:T(8,128)}, f32[1024,256]{1,0:T(8,128)}, u32[]{:S(2)}, u32[]{:S(2)}) collective-permute-start(f32[1024,256]{1,0:T(8,128)} %get-tuple-element.156), channel_id=1, source_target_pairs={{0,1},{1,2},{2,3},{3,4},{4,5},{5,6},{6,7},{7,8},{8,9},{9,10},{10,1... | collective-permute-start | bytes 3145736 | tf_op jit(solution)/shard_map/ppermute | solution.py:22
  189.5 16.4 %collective-permute-start.2 = (f32[1024,256]{1,0:T(8,128)}, f32[1024,256]{1,0:T(8,128)}, u32[]{:S(2)}, u32[]{:S(2)}) collective-permute-start(f32[1024,256]{1,0:T(8,128)} %get-tuple-element.155), channel_id=1, source_target_pairs={{1,0},{2,1},{3,2},{4,3},{5,4},{6,5},{7,6},{8,7},{9,8},{10,9},{11,1... | collective-permute-start | bytes 3145736 | tf_op jit(solution)/shard_map/ppermute | solution.py:22
  210.0 4.7 %copy-start.6 = (f32[8,64,512]{2,1,0:T(8,128)S(1)}, f32[8,64,512]{2,1,0:T(8,128)}, u32[]{:S(2)}) copy-start(f32[8,64,512]{2,1,0:T(8,128)} %copy-done.4) | copy-start | bytes 3145732
  210.0 36.0 %all-to-all-start.3 = ((f32[8,256,256]{2,1,0:T(8,128)}), f32[8,256,256]{2,1,0:T(8,128)}, u32[]{:S(2)}, u32[]{:S(2)}) async-start(f32[8,256,256]{2,1,0:T(8,128)} %broadcast_in_dim.7), calls=%async_computation.3 | async-start | bytes 4194304 | tf_op jit(solution)/shard_map/all_to_all | solution.py:88
  217.0 5.2 %collective-permute-start.1 = (f32[256,256]{1,0:T(8,128)S(1)}, f32[256,256]{1,0:T(8,128)S(1)}, u32[]{:S(2)}, u32[]{:S(2)}) collective-permute-start(f32[256,256]{1,0:T(8,128)S(1)} %get-tuple-element.166), channel_id=1, source_target_pairs={{0,1},{1,2},{2,3},{3,4},{4,5},{5,6},{6,7},{7,8},{8,9},{9,10},{10,1... | collective-permute-start | bytes 786440 | tf_op jit(solution)/shard_map/ppermute | solution.py:22
  218.9 8.1 %collective-permute-start.3 = (f32[256,256]{1,0:T(8,128)S(1)}, f32[256,256]{1,0:T(8,128)S(1)}, u32[]{:S(2)}, u32[]{:S(2)}) collective-permute-start(f32[256,256]{1,0:T(8,128)S(1)} %get-tuple-element.167), channel_id=1, source_target_pairs={{1,0},{2,1},{3,2},{4,3},{5,4},{6,5},{7,6},{8,7},{9,8},{10,9},{11,1... | collective-permute-start | bytes 786440 | tf_op jit(solution)/shard_map/ppermute | solution.py:22
  227.0 23.1 %copy-start.13 = (f32[256,256]{1,0:T(8,128)}, f32[256,256]{1,0:T(8,128)S(1)}, u32[]{:S(2)}) copy-start(f32[256,256]{1,0:T(8,128)S(1)} %get-tuple-element.161) | copy-start | bytes 786436
  227.1 23.1 %copy-start.15 = (f32[256,256]{1,0:T(8,128)}, f32[256,256]{1,0:T(8,128)S(1)}, u32[]{:S(2)}) copy-start(f32[256,256]{1,0:T(8,128)S(1)} %get-tuple-element.162) | copy-start | bytes 786436
  247.9 2.3 copy-start.11
  250.1 3.6 %copy-start.9 = (f32[512,512]{1,0:T(8,128)}, f32[512,512]{1,0:T(8,128)S(1)}, u32[]{:S(2)}) copy-start(f32[512,512]{1,0:T(8,128)S(1)} %get-tuple-element.168) | copy-start | bytes 3145732
  285.1 1.2 copy-start.10
  285.1 1.3 copy-start.12
  285.1 1.3 copy-start.14
  285.1 1.4 copy-start.16
  286.5 2.2 copy-start.3
